TPU v7x, 768 devices: a whole 4x8x12 slice. The times are simulated.
768 devices in a mesh: dp: 64 (over y, z_hi, core), block: 12 (over z_lo, x).
Axes of the slice: x: 4, y: 8, z: 12 (z_hi: 4, z_lo: 3; z = z_hi * 3 + z_lo), core: 2. Of those that a mesh axis runs over, the one named last changes fastest.
Arguments:
- tokens: bfloat16 [18432, 6144], P('dp', 'block'), may hold values from -6 to 6
- up_first: bfloat16 [96, 64, 256], P('block'), may hold values from -0.75 to 0.75
- up_mix: bfloat16 [256, 96, 96], replicated, may hold values from -0.625 to 0.625
- down_mix: bfloat16 [256, 96, 96], replicated, may hold values from -0.625 to 0.625
- down_last: bfloat16 [96, 64, 256], P('block'), may hold values from -0.375 to 0.375
- cotangent: bfloat16 [18432, 6144], P('dp', 'block'), may hold values from -6 to 6
Outputs:
- encoded: bfloat16 [18432, 6144], P('dp', 'block')
- grad_tokens: bfloat16 [18432, 6144], P('dp', 'block')
- grad_up_first: float32 [96, 64, 256], P('block')
- grad_down_last: float32 [96, 64, 256], P('block')
All inputs are finite; a program needn't handle non-finite values.
Results may differ from a plain program's by a relative error of at most 0.014.
Values may be sent and summed in bfloat16 or wider, within the bound.
No kernel may reach another device: no remote copies, remote signals or barrier semaphores. Data moves between devices by JAX's collectives and lax.ppermute only.
A program may use at most 64 MiB of HBM per device.

v0:
```python
import jax
import jax.numpy as jnp
from jax import lax
from jax.sharding import PartitionSpec as P

gelu_coef = 0.7978845608028654
cubic_coef = 0.044715


def gelu_pair(values):
    inner = gelu_coef * (values + cubic_coef * values * values * values)
    tangent = jnp.tanh(inner)
    result = 0.5 * values * (1.0 + tangent)
    slope = 0.5 * (1.0 + tangent) + 0.5 * values * (1.0 - tangent * tangent) * gelu_coef * (
        1.0 + 3.0 * cubic_coef * values * values
    )
    return (result, slope)


def to_tokens(panel):
    return lax.all_to_all(panel, "block", split_axis=0, concat_axis=1, tiled=True)


def to_blocks(panel):
    return lax.all_to_all(panel, "block", split_axis=1, concat_axis=0, tiled=True)


def shards(tokens, up_first, up_mix, down_mix, down_last, cotangent):
    flt = jnp.float32
    half = jnp.bfloat16
    row_count = tokens.shape[0]
    local_blocks = up_first.shape[0]
    width_in = up_first.shape[1]
    inputs = tokens.reshape(row_count, local_blocks, width_in)
    outgrads = cotangent.reshape(row_count, local_blocks, width_in)
    first = jnp.einsum("trk,rkc->trc", inputs, up_first, preferred_element_type=flt).astype(half)
    grad_mixed = jnp.einsum("tqk,qkc->tqc", outgrads, down_last, preferred_element_type=flt).astype(
        half
    )
    first_tok = to_tokens(first)
    pre_tok = jnp.einsum("trc,csr->tsc", first_tok, up_mix, preferred_element_type=flt).astype(half)
    hidden_f, slope = gelu_pair(pre_tok.astype(flt))
    hidden_tok = hidden_f.astype(half)
    mixed_tok = jnp.einsum("tsc,cqs->tqc", hidden_tok, down_mix, preferred_element_type=flt).astype(
        half
    )
    mixed = to_blocks(mixed_tok)
    encoded = jnp.einsum("tqc,qkc->tqk", mixed, down_last, preferred_element_type=flt).astype(half)
    grad_last = jnp.einsum("tqk,tqc->qkc", outgrads, mixed, preferred_element_type=flt)
    grad_mixed_tok = to_tokens(grad_mixed)
    grad_hidden_tok = jnp.einsum(
        "tqc,cqs->tsc", grad_mixed_tok, down_mix, preferred_element_type=flt
    ).astype(half)
    grad_pre_tok = (grad_hidden_tok.astype(flt) * slope).astype(half)
    grad_first_tok = jnp.einsum(
        "tsc,csr->trc", grad_pre_tok, up_mix, preferred_element_type=flt
    ).astype(half)
    grad_first = to_blocks(grad_first_tok)
    grad_in = jnp.einsum("trc,rkc->trk", grad_first, up_first, preferred_element_type=flt).astype(
        half
    )
    grad_firstw = jnp.einsum("trk,trc->rkc", inputs, grad_first, preferred_element_type=flt)
    summed_first, summed_last = lax.psum((grad_firstw, grad_last), "dp")
    return (
        encoded.reshape(row_count, local_blocks * width_in),
        grad_in.reshape(row_count, local_blocks * width_in),
        summed_first,
        summed_last,
    )


def solution(mesh):
    placed = (
        P("dp", "block"),
        P("block", None, None),
        P(),
        P(),
        P("block", None, None),
        P("dp", "block"),
    )
    return jax.shard_map(
        shards,
        mesh=mesh,
        in_specs=placed,
        out_specs=(
            P("dp", "block"),
            P("dp", "block"),
            P("block", None, None),
            P("block", None, None),
        ),
        check_vma=False,
    )
```

profile of v0, /device:TPU:7, one launch (start us, length us, event | category | flops | bytes accessed | tf_op | source)
XLA Modules:
  0.0 785.2 jit_solution(7407118431829162358)
XLA Ops:
  7.2 0.0 copy-start
  7.2 1.2 copy.63
  8.4 0.0 copy-done
  8.4 0.0 copy-start.2
  8.4 0.5 fusion.29
  8.9 0.0 copy-start.1
  9.0 1.7 copy.64
  10.6 7.8 all-to-all-start.2
  18.5 0.0 copy-done.2
  18.5 0.2 copy.54
  18.7 0.0 copy-done.1
  18.7 0.5 fusion.28
  19.2 1.7 copy.55
  20.9 12.6 %all-to-all-done.2 = bf16[288,8,256]{2,1,0:T(8,128)(2,1)S(1)} async-done(((bf16[288,8,256]{2,1,0:T(8,128)(2,1)}), bf16[288,8,256]{2,1,0:T(8,128)(2,1)S(1)}, u32[]{:S(2)}, u32[]{:S(2)}) %all-to-all-start.2) | async-done | bytes 1179680 | tf_op jit(solution)/shard_map/all_to_all | solution.py:21
  33.5 8.2 %all-to-all-start = ((bf16[288,8,256]{2,1,0:T(8,128)(2,1)}), bf16[288,8,256]{2,1,0:T(8,128)(2,1)S(1)}, u32[]{:S(2)}, u32[]{:S(2)}) async-start(bf16[288,8,256]{2,1,0:T(8,128)(2,1)} %copy.55), calls=%async_computation | async-start | bytes 2359296 | tf_op jit(solution)/shard_map/all_to_all | solution.py:21
  41.7 8.5 %copy.58 = bf16[256,96,96]{2,1,0:T(8,128)(2,1)} copy(bf16[256,96,96]{0,2,1:T(8,128)(2,1)} %param.8) | data formatting | bytes 9437184 | tf_op args[2]
  50.2 8.5 %copy.59 = bf16[256,96,96]{2,1,0:T(8,128)(2,1)} copy(bf16[256,96,96]{0,2,1:T(8,128)(2,1)} %param.9) | data formatting | bytes 9437184 | tf_op args[3]
  58.7 1.2 copy.78
  59.9 2.7 copy.66
  62.6 0.0 all-to-all-done
  62.6 1.2 copy.79
  63.8 1.9 copy.57
  65.7 7.3 convolution_convert_fusion.3
  73.0 9.9 %fusion.25 = bf16[24,96,256]{1,0,2:T(8,128)(2,1)S(1)} fusion(bf16[256,96,96]{2,1,0:T(8,128)(2,1)} %copy.58, bf16[256,24,96]{2,1,0:T(8,128)(2,1)} %convolution_convert_fusion.3, bf16[24,96,256]{1,0,2:T(8,128)(2,1)} %copy.66, bf16[256,96,96]{2,1,0:T(8,128)(2,1)} %copy.59), kind=kOutput, calls=%fused_computation.30 | convolution fusion | flops 240058368 | bytes 12976128 | tf_op jit(solution)/shard_map/tsc,csr->trc/dot_general | solution.py:55
  82.9 2.1 copy.69
  85.0 6.0 all-to-all-start.3
  91.1 7.8 fusion.22
  98.8 3.2 copy.60
  102.0 5.9 all-to-all-done.3
  107.9 8.4 %all-to-all-start.1 = ((bf16[24,96,256]{2,0,1:T(8,128)(2,1)}), bf16[24,96,256]{2,0,1:T(8,128)(2,1)}, u32[]{:S(2)}, u32[]{:S(2)}) async-start(bf16[24,96,256]{2,0,1:T(8,128)(2,1)} %copy.60), calls=%async_computation.1 | async-start | bytes 2359296 | tf_op jit(solution)/shard_map/all_to_all | solution.py:25
  116.3 0.0 all-reduce.3.cloned.1.call-start
  116.3 0.1 copy.71
  116.4 18.3 %all-to-all-done.1 = bf16[24,96,256]{2,0,1:T(8,128)(2,1)} async-done(((bf16[24,96,256]{2,0,1:T(8,128)(2,1)}), bf16[24,96,256]{2,0,1:T(8,128)(2,1)}, u32[]{:S(2)}, u32[]{:S(2)}) %all-to-all-start.1) | async-done | bytes 1179680 | tf_op jit(solution)/shard_map/all_to_all | solution.py:25
  134.7 1.4 copy.62
  136.1 1.2 convolution_bitcast_fusion
  137.3 1.2 convolution_bitcast_fusion.1
  138.4 0.0 all-reduce.3.cloned.1.call-update
  138.5 0.5 convolution_convert_fusion.7
  139.0 0.9 copy.72
  139.8 1.4 convolution_convert_fusion.6
  141.3 0.9 copy.73
  142.2 632.4 %all-reduce.3.cloned.1.call-done = (f32[8,64,256]{2,1,0:T(8,128)}, f32[8,64,256]{2,1,0:T(8,128)}) async-done(((f32[8,64,256]{2,1,0:T(8,128)}, f32[8,64,256]{2,1,0:T(8,128)}), (f32[8,64,256]{2,1,0:T(8,128)}, f32[8,64,256]{2,1,0:T(8,128)})) %all-reduce.3.cloned.1.call-update) | async-done | bytes 1048592 | tf_op jit(solution)/shard_map/psum | solution.py:63
  774.6 1.9 copy.82
  776.4 1.9 copy.83
Async XLA Ops:
  7.2 1.2 copy-start
  8.4 10.1 %copy-start.2 = (bf16[288,512]{1,0:T(8,128)(2,1)S(1)}, bf16[288,512]{1,0:T(8,128)(2,1)}, u32[]{:S(2)}) copy-start(bf16[288,512]{1,0:T(8,128)(2,1)} %param.6) | copy-start | bytes 884740
  8.9 9.8 %copy-start.1 = (bf16[8,64,256]{2,1,0:T(8,128)(2,1)S(1)}, bf16[8,64,256]{2,1,0:T(8,128)(2,1)}, u32[]{:S(2)}) copy-start(bf16[8,64,256]{2,1,0:T(8,128)(2,1)} %param.7) | copy-start | bytes 786436
  10.6 22.9 %all-to-all-start.2 = ((bf16[288,8,256]{2,1,0:T(8,128)(2,1)}), bf16[288,8,256]{2,1,0:T(8,128)(2,1)S(1)}, u32[]{:S(2)}, u32[]{:S(2)}) async-start(bf16[288,8,256]{2,1,0:T(8,128)(2,1)} %copy.64), calls=%async_computation.2 | async-start | bytes 2359296 | tf_op jit(solution)/shard_map/all_to_all | solution.py:21
  33.5 29.1 %all-to-all-start = ((bf16[288,8,256]{2,1,0:T(8,128)(2,1)}), bf16[288,8,256]{2,1,0:T(8,128)(2,1)S(1)}, u32[]{:S(2)}, u32[]{:S(2)}) async-start(bf16[288,8,256]{2,1,0:T(8,128)(2,1)} %copy.55), calls=%async_computation | async-start | bytes 2359296 | tf_op jit(solution)/shard_map/all_to_all | solution.py:21
  85.0 22.9 %all-to-all-start.3 = ((bf16[24,96,256]{2,0,1:T(8,128)(2,1)}), bf16[24,96,256]{2,0,1:T(8,128)(2,1)S(1)}, u32[]{:S(2)}, u32[]{:S(2)}) async-start(bf16[24,96,256]{2,0,1:T(8,128)(2,1)} %copy.69), calls=%async_computation.3 | async-start | bytes 2359296 | tf_op jit(solution)/shard_map/all_to_all | solution.py:25
  107.9 26.8 %all-to-all-start.1 = ((bf16[24,96,256]{2,0,1:T(8,128)(2,1)}), bf16[24,96,256]{2,0,1:T(8,128)(2,1)}, u32[]{:S(2)}, u32[]{:S(2)}) async-start(bf16[24,96,256]{2,0,1:T(8,128)(2,1)} %copy.60), calls=%async_computation.1 | async-start | bytes 2359296 | tf_op jit(solution)/shard_map/all_to_all | solution.py:25
  116.3 658.3 %all-reduce.3.cloned.1.call-start = ((), (), s32[]{:S(2)}) async-start(), calls=%async_computation.4 | async-start | bytes 2097152 | tf_op jit(solution)/shard_map/psum | solution.py:63
Sparse Core Ops, SparseCore 0:
  138.6 635.9 all-reduce.2
where the time goes:
time: 788 us; the launch traced here: 785 us
  waiting for transfers between devices  669 us (85%)
  local copies, waits for them, and re-layouts  41 us (5%)
  starting transfers between devices  30.5 us (4%)
  matrix products  30.2 us (4%)
  between operations  14.1 us (2%)
    psum x1, waiting for transfers between devices, shards(): summed_first, summed_last = lax.psum((grad_firstw, grad_last), 'dp')  632 us
    all_to_all x2, waiting for transfers between devices, to_blocks(): lax.all_to_all(panel, 'block', split_axis=1, concat_axis=0, tiled=True)  24.2 us
    unnamed x14, local copies, waits for them, and re-layouts  24 us
    all_to_all x2, starting transfers between devices, to_tokens(): lax.all_to_all(panel, 'block', split_axis=0, concat_axis=1, tiled=True)  16.1 us
  transfers between devices with their start and end apart: 5, of which 4 were waited for; matrix products, arithmetic and copies ran while one was open for 5% of the time, Pallas kernels for 0%

commit v1 on v0

--- a/solution.py
+++ b/solution.py
@@ -1,7 +1,9 @@
 import jax
 import jax.numpy as jnp
 from jax import lax
-from jax.sharding import PartitionSpec as P
+from jax.sharding import PartitionSpec as P, Mesh
+DP = ("y", "zh", "core")
+BLK = ("zl", "x")
 
 gelu_coef = 0.7978845608028654
 cubic_coef = 0.044715
@@ -18,11 +20,11 @@
 
 
 def to_tokens(panel):
-    return lax.all_to_all(panel, "block", split_axis=0, concat_axis=1, tiled=True)
+    return lax.all_to_all(panel, BLK, split_axis=0, concat_axis=1, tiled=True)
 
 
 def to_blocks(panel):
-    return lax.all_to_all(panel, "block", split_axis=1, concat_axis=0, tiled=True)
+    return lax.all_to_all(panel, BLK, split_axis=1, concat_axis=0, tiled=True)
 
 
 def shards(tokens, up_first, up_mix, down_mix, down_last, cotangent):
@@ -60,7 +62,13 @@
         half
     )
     grad_firstw = jnp.einsum("trk,trc->rkc", inputs, grad_first, preferred_element_type=flt)
-    summed_first, summed_last = lax.psum((grad_firstw, grad_last), "dp")
+
+    both = jnp.concatenate([grad_firstw.reshape(-1, grad_firstw.shape[-1]), grad_last.reshape(-1, grad_last.shape[-1])], axis=0)
+    both = lax.psum_scatter(both, DP, scatter_dimension=0, tiled=True)
+    both = lax.all_gather(both, DP, axis=0, tiled=True)
+    summed_first, summed_last = jnp.split(both, 2, axis=0)
+    summed_first = summed_first.reshape(grad_firstw.shape)
+    summed_last = summed_last.reshape(grad_last.shape)
     return (
         encoded.reshape(row_count, local_blocks * width_in),
         grad_in.reshape(row_count, local_blocks * width_in),
@@ -70,23 +78,24 @@
 
 
 def solution(mesh):
+    mesh = Mesh(mesh.devices.reshape(8, 4, 2, 3, 4), ("y", "zh", "core", "zl", "x"))
     placed = (
-        P("dp", "block"),
-        P("block", None, None),
+        P(DP, BLK),
+        P(BLK, None, None),
         P(),
         P(),
-        P("block", None, None),
-        P("dp", "block"),
+        P(BLK, None, None),
+        P(DP, BLK),
     )
     return jax.shard_map(
         shards,
         mesh=mesh,
         in_specs=placed,
         out_specs=(
-            P("dp", "block"),
-            P("dp", "block"),
-            P("block", None, None),
-            P("block", None, None),
+            P(DP, BLK),
+            P(DP, BLK),
+            P(BLK, None, None),
+            P(BLK, None, None),
         ),
         check_vma=False,
     )

time: 788 us -> 415 us (0.53)
  waiting for transfers between devices: 669 us -> 300 us
    psum x1 -> x0, waiting for transfers between devices: 632 us -> none  [shards(): summed_first, summed_last = lax.psum((grad_firstw, grad_last), 'dp')]
    reduce_scatter x0 -> x1, waiting for transfers between devices: none -> 171 us  [shards(): both = lax.psum_scatter(both, DP, scatter_dimension=0, tiled=True)]
    all_gather x0 -> x1, waiting for transfers between devices: none -> 92.5 us  [shards(): both = lax.all_gather(both, DP, axis=0, tiled=True)]
  transfers between devices with their start and end apart: 5 -> 6, of which waited for: 4 -> 5; matrix products, arithmetic and copies ran while one was open for 5% -> 9% of each run, Pallas kernels for 0% -> 0%
where the time goes in v1:
time: 415 us; the launch traced here: 413 us
  waiting for transfers between devices  300 us (72%)
  local copies, waits for them, and re-layouts  39.5 us (10%)
  starting transfers between devices  30.5 us (7%)
  matrix products  27.7 us (7%)
  between operations  14.2 us (3%)
    reduce_scatter x1, waiting for transfers between devices, shards(): both = lax.psum_scatter(both, DP, scatter_dimension=0, tiled=True)  171 us
    all_gather x1, waiting for transfers between devices, shards(): both = lax.all_gather(both, DP, axis=0, tiled=True)  92.5 us
    all_to_all x2, waiting for transfers between devices, to_blocks(): return lax.all_to_all(panel, BLK, split_axis=1, concat_axis=0, tiled=True)  24.2 us
    unnamed x14, local copies, waits for them, and re-layouts  20.2 us
    all_to_all x2, starting transfers between devices, to_tokens(): return lax.all_to_all(panel, BLK, split_axis=0, concat_axis=1, tiled=True)  16.1 us
    all_to_all x2, starting transfers between devices, to_blocks(): return lax.all_to_all(panel, BLK, split_axis=1, concat_axis=0, tiled=True)  14.4 us
    all_to_all x2, waiting for transfers between devices, to_tokens(): return lax.all_to_all(panel, BLK, split_axis=0, concat_axis=1, tiled=True)  12.6 us
    dot_general x1, matrix products, shards(): jnp.einsum('tsc,csr->trc', grad_pre_tok, up_mix, preferred_element_type=flt)  9.86 us
  transfers between devices with their start and end apart: 6, of which 5 were waited for; matrix products, arithmetic and copies ran while one was open for 9% of the time, Pallas kernels for 0%

profile of v1, /device:TPU:7, one launch (start us, length us, event | category | flops | bytes accessed | tf_op | source)
XLA Modules:
  0.0 413.4 jit_solution(17583721817814620923)
XLA Ops:
  7.2 0.0 copy-start
  7.2 1.2 copy.63
  8.4 0.0 copy-done
  8.4 0.0 copy-start.3
  8.4 0.5 fusion.29
  8.9 0.0 copy-start.1
  9.0 1.7 copy.64
  10.6 7.8 %all-to-all-start.2 = ((bf16[288,8,256]{2,1,0:T(8,128)(2,1)}), bf16[288,8,256]{2,1,0:T(8,128)(2,1)S(1)}, u32[]{:S(2)}, u32[]{:S(2)}) async-start(bf16[288,8,256]{2,1,0:T(8,128)(2,1)} %copy.64), calls=%async_computation.2 | async-start | bytes 2359296 | tf_op jit(solution)/shard_map/all_to_all | solution.py:23
  18.5 0.0 copy-done.3
  18.5 0.2 copy.54
  18.7 0.0 copy-done.1
  18.7 0.5 fusion.28
  19.2 1.7 copy.55
  20.9 12.6 %all-to-all-done.2 = bf16[288,8,256]{2,1,0:T(8,128)(2,1)S(1)} async-done(((bf16[288,8,256]{2,1,0:T(8,128)(2,1)}), bf16[288,8,256]{2,1,0:T(8,128)(2,1)S(1)}, u32[]{:S(2)}, u32[]{:S(2)}) %all-to-all-start.2) | async-done | bytes 1179680 | tf_op jit(solution)/shard_map/all_to_all | solution.py:23
  33.5 8.2 %all-to-all-start = ((bf16[288,8,256]{2,1,0:T(8,128)(2,1)}), bf16[288,8,256]{2,1,0:T(8,128)(2,1)S(1)}, u32[]{:S(2)}, u32[]{:S(2)}) async-start(bf16[288,8,256]{2,1,0:T(8,128)(2,1)} %copy.55), calls=%async_computation | async-start | bytes 2359296 | tf_op jit(solution)/shard_map/all_to_all | solution.py:23
  41.7 8.5 %copy.58 = bf16[256,96,96]{2,1,0:T(8,128)(2,1)} copy(bf16[256,96,96]{0,2,1:T(8,128)(2,1)} %param.8) | data formatting | bytes 9437184 | tf_op args[2]
  50.3 8.5 %copy.59 = bf16[256,96,96]{2,1,0:T(8,128)(2,1)} copy(bf16[256,96,96]{0,2,1:T(8,128)(2,1)} %param.9) | data formatting | bytes 9437184 | tf_op args[3]
  58.7 1.2 copy.78
  59.9 2.7 copy.66
  62.6 0.0 all-to-all-done
  62.6 1.1 copy.79
  63.7 1.9 copy.57
  65.7 7.3 %convolution_convert_fusion.3 = bf16[256,24,96]{2,1,0:T(8,128)(2,1)} fusion(bf16[24,96,256]{1,0,2:T(8,128)(2,1)S(1)} %copy.57, bf16[256,96,96]{2,1,0:T(8,128)(2,1)} %copy.58), kind=kOutput, calls=%fused_computation.17 | convolution fusion | flops 113836032 | bytes 7077888 | tf_op jit(solution)/shard_map/trc,csr->tsc/dot_general | solution.py:43
  73.0 9.9 %fusion.25 = bf16[24,96,256]{1,0,2:T(8,128)(2,1)S(1)} fusion(bf16[256,96,96]{2,1,0:T(8,128)(2,1)} %copy.58, bf16[256,24,96]{2,1,0:T(8,128)(2,1)} %convolution_convert_fusion.3, bf16[24,96,256]{1,0,2:T(8,128)(2,1)} %copy.66, bf16[256,96,96]{2,1,0:T(8,128)(2,1)} %copy.59), kind=kOutput, calls=%fused_computation.30 | convolution fusion | flops 240058368 | bytes 12976128 | tf_op jit(solution)/shard_map/tsc,csr->trc/dot_general | solution.py:57
  82.8 2.1 copy.69
  85.0 6.0 %all-to-all-start.3 = ((bf16[24,96,256]{2,0,1:T(8,128)(2,1)}), bf16[24,96,256]{2,0,1:T(8,128)(2,1)S(1)}, u32[]{:S(2)}, u32[]{:S(2)}) async-start(bf16[24,96,256]{2,0,1:T(8,128)(2,1)} %copy.69), calls=%async_computation.3 | async-start | bytes 2359296 | tf_op jit(solution)/shard_map/all_to_all | solution.py:27
  91.0 7.8 %fusion.22 = bf16[24,96,256]{1,0,2:T(8,128)(2,1)} fusion(bf16[256,96,96]{2,1,0:T(8,128)(2,1)} %copy.59, bf16[256,24,96]{2,1,0:T(8,128)(2,1)} %convolution_convert_fusion.3), kind=kOutput, calls=%fused_computation.29 | convolution fusion | flops 119734272 | bytes 7077888 | tf_op jit(solution)/shard_map/tsc,cqs->tqc/dot_general | solution.py:46
  98.8 3.2 copy.60
  102.0 5.9 %all-to-all-done.3 = bf16[24,96,256]{2,0,1:T(8,128)(2,1)S(1)} async-done(((bf16[24,96,256]{2,0,1:T(8,128)(2,1)}), bf16[24,96,256]{2,0,1:T(8,128)(2,1)S(1)}, u32[]{:S(2)}, u32[]{:S(2)}) %all-to-all-start.3) | async-done | bytes 1179680 | tf_op jit(solution)/shard_map/all_to_all | solution.py:27
  107.9 8.4 %all-to-all-start.1 = ((bf16[24,96,256]{2,0,1:T(8,128)(2,1)}), bf16[24,96,256]{2,0,1:T(8,128)(2,1)}, u32[]{:S(2)}, u32[]{:S(2)}) async-start(bf16[24,96,256]{2,0,1:T(8,128)(2,1)} %copy.60), calls=%async_computation.1 | async-start | bytes 2359296 | tf_op jit(solution)/shard_map/all_to_all | solution.py:27
  116.3 0.0 reduce-scatter.2.cloned.1.call-start
  116.3 0.1 copy.71
  116.4 18.3 %all-to-all-done.1 = bf16[24,96,256]{2,0,1:T(8,128)(2,1)} async-done(((bf16[24,96,256]{2,0,1:T(8,128)(2,1)}), bf16[24,96,256]{2,0,1:T(8,128)(2,1)}, u32[]{:S(2)}, u32[]{:S(2)}) %all-to-all-start.1) | async-done | bytes 1179680 | tf_op jit(solution)/shard_map/all_to_all | solution.py:27
  134.7 1.4 copy.62
  136.1 0.4 fusion.41
  136.4 0.4 fusion.40
  136.8 0.0 copy-start.2
  136.8 1.0 pad_maximum_fusion
  137.9 0.0 reduce-scatter.2.cloned.1.call-update
  137.9 0.0 all-gather.2.cloned.1.call-start
  138.0 171.1 %reduce-scatter.2.cloned.1.call-done = f32[16,256]{1,0:T(8,128)} async-done(((f32[1024,256]{1,0:T(8,128)}), f32[16,256]{1,0:T(8,128)}) %reduce-scatter.2.cloned.1.call-update) | async-done | bytes 16400 | tf_op jit(solution)/shard_map/reduce_scatter | solution.py:67
  309.0 0.0 all-gather.2.cloned.1.call-update
  309.0 0.5 convolution_convert_fusion.7
  309.5 0.9 copy.72
  310.4 0.5 convolution_convert_fusion.6
  310.9 0.9 copy.73
  311.8 92.5 %all-gather.2.cloned.1.call-done = f32[1024,256]{1,0:T(8,128)} async-done(((f32[16,256]{1,0:T(8,128)}), f32[1024,256]{1,0:T(8,128)}) %all-gather.2.cloned.1.call-update) | async-done | bytes 1048592 | tf_op jit(solution)/shard_map/all_gather | solution.py:68
  404.3 2.2 fusion.39
  (1 shorter events, 0.0 us)
Async XLA Ops:
  7.2 1.2 copy-start
  8.4 10.1 %copy-start.3 = (bf16[288,512]{1,0:T(8,128)(2,1)S(1)}, bf16[288,512]{1,0:T(8,128)(2,1)}, u32[]{:S(2)}) copy-start(bf16[288,512]{1,0:T(8,128)(2,1)} %param.6) | copy-start | bytes 884740
  8.9 9.8 %copy-start.1 = (bf16[8,64,256]{2,1,0:T(8,128)(2,1)S(1)}, bf16[8,64,256]{2,1,0:T(8,128)(2,1)}, u32[]{:S(2)}) copy-start(bf16[8,64,256]{2,1,0:T(8,128)(2,1)} %param.7) | copy-start | bytes 786436
  10.6 22.9 %all-to-all-start.2 = ((bf16[288,8,256]{2,1,0:T(8,128)(2,1)}), bf16[288,8,256]{2,1,0:T(8,128)(2,1)S(1)}, u32[]{:S(2)}, u32[]{:S(2)}) async-start(bf16[288,8,256]{2,1,0:T(8,128)(2,1)} %copy.64), calls=%async_computation.2 | async-start | bytes 2359296 | tf_op jit(solution)/shard_map/all_to_all | solution.py:23
  33.5 29.1 %all-to-all-start = ((bf16[288,8,256]{2,1,0:T(8,128)(2,1)}), bf16[288,8,256]{2,1,0:T(8,128)(2,1)S(1)}, u32[]{:S(2)}, u32[]{:S(2)}) async-start(bf16[288,8,256]{2,1,0:T(8,128)(2,1)} %copy.55), calls=%async_computation | async-start | bytes 2359296 | tf_op jit(solution)/shard_map/all_to_all | solution.py:23
  85.0 22.9 %all-to-all-start.3 = ((bf16[24,96,256]{2,0,1:T(8,128)(2,1)}), bf16[24,96,256]{2,0,1:T(8,128)(2,1)S(1)}, u32[]{:S(2)}, u32[]{:S(2)}) async-start(bf16[24,96,256]{2,0,1:T(8,128)(2,1)} %copy.69), calls=%async_computation.3 | async-start | bytes 2359296 | tf_op jit(solution)/shard_map/all_to_all | solution.py:27
  107.9 26.8 %all-to-all-start.1 = ((bf16[24,96,256]{2,0,1:T(8,128)(2,1)}), bf16[24,96,256]{2,0,1:T(8,128)(2,1)}, u32[]{:S(2)}, u32[]{:S(2)}) async-start(bf16[24,96,256]{2,0,1:T(8,128)(2,1)} %copy.60), calls=%async_computation.1 | async-start | bytes 2359296 | tf_op jit(solution)/shard_map/all_to_all | solution.py:27
  116.3 192.8 %reduce-scatter.2.cloned.1.call-start = ((), (), s32[]{:S(2)}) async-start(), calls=%async_computation.5 | async-start | bytes 1064960 | tf_op jit(solution)/shard_map/reduce_scatter | solution.py:67
  136.8 173.6 %copy-start.2 = (bf16[8,64,256]{2,1,0:T(8,128)(2,1)S(1)}, bf16[8,64,256]{2,1,0:T(8,128)(2,1)}, u32[]{:S(2)}) copy-start(bf16[8,64,256]{2,1,0:T(8,128)(2,1)} %param.7) | copy-start | bytes 786436
  137.9 266.4 %all-gather.2.cloned.1.call-start = ((), (), s32[]{:S(2)}) async-start(), calls=%async_computation.6 | async-start | bytes 1064960 | tf_op jit(solution)/shard_map/all_gather | solution.py:68
Sparse Core Ops, SparseCore 0:
  138.0 170.9 reduce-scatter.1
  312.9 91.3 all-gather.1

commit v2 on v1

--- a/solution.py
+++ b/solution.py
@@ -64,8 +64,10 @@
     grad_firstw = jnp.einsum("trk,trc->rkc", inputs, grad_first, preferred_element_type=flt)
 
     both = jnp.concatenate([grad_firstw.reshape(-1, grad_firstw.shape[-1]), grad_last.reshape(-1, grad_last.shape[-1])], axis=0)
-    both = lax.psum_scatter(both, DP, scatter_dimension=0, tiled=True)
-    both = lax.all_gather(both, DP, axis=0, tiled=True)
+    parts = lax.all_to_all(both.reshape(64, -1, both.shape[-1]), DP, 0, 0, tiled=True)
+    part = parts.sum(axis=0)
+    spread = jnp.broadcast_to(part[None], (64,) + part.shape)
+    both = lax.all_to_all(spread, DP, 0, 0, tiled=True).reshape(-1, part.shape[-1])
     summed_first, summed_last = jnp.split(both, 2, axis=0)
     summed_first = summed_first.reshape(grad_firstw.shape)
     summed_last = summed_last.reshape(grad_last.shape)

time: 415 us -> 264 us (0.64)
  waiting for transfers between devices: 300 us -> 76.2 us
  blocking collectives: 0 us -> 75.7 us
  between operations: 14.2 us -> 0.78 us
  starting transfers between devices: 30.5 us -> 37.1 us
    reduce_scatter x1 -> x0, waiting for transfers between devices: 171 us -> none  [shards(): both = lax.psum_scatter(both, DP, scatter_dimension=0, tiled=True)]
    all_gather x1 -> x0, waiting for transfers between devices: 92.5 us -> none  [shards(): both = lax.all_gather(both, DP, axis=0, tiled=True)]
    all_to_all x0 -> x1, blocking collectives: none -> 75.7 us  [shards(): lax.all_to_all(both.reshape(64, -1, both.shape[-1]), DP, 0, 0, tiled=True)]
    all_to_all x0 -> x1, waiting for transfers between devices: none -> 39.4 us  [shards(): lax.all_to_all(spread, DP, 0, 0, tiled=True).reshape(-1, part.shape[-1])]
    all_to_all x0 -> x1, starting transfers between devices: none -> 6.59 us  [shards(): lax.all_to_all(spread, DP, 0, 0, tiled=True).reshape(-1, part.shape[-1])]
  transfers between devices with their start and end apart: 6 -> 5, of which waited for: 5 -> 4; matrix products, arithmetic and copies ran while one was open for 9% -> 14% of each run, Pallas kernels for 0% -> 0%
where the time goes in v2:
time: 264 us; the launch traced here: 260 us
  waiting for transfers between devices  76.2 us (29%)
  blocking collectives  75.7 us (29%)
  local copies, waits for them, and re-layouts  40.6 us (15%)
  starting transfers between devices  37.1 us (14%)
  matrix products  27.7 us (10%)
    all_to_all x1, blocking collectives, shards(): lax.all_to_all(both.reshape(64, -1, both.shape[-1]), DP, 0, 0, tiled=True)  75.7 us
    all_to_all x1, waiting for transfers between devices, shards(): lax.all_to_all(spread, DP, 0, 0, tiled=True).reshape(-1, part.shape[-1])  39.4 us
    all_to_all x2, waiting for transfers between devices, to_blocks(): return lax.all_to_all(panel, BLK, split_axis=1, concat_axis=0, tiled=True)  24.2 us
    unnamed x14, local copies, waits for them, and re-layouts  20.1 us
    all_to_all x2, starting transfers between devices, to_tokens(): return lax.all_to_all(panel, BLK, split_axis=0, concat_axis=1, tiled=True)  16.1 us
    all_to_all x2, starting transfers between devices, to_blocks(): return lax.all_to_all(panel, BLK, split_axis=1, concat_axis=0, tiled=True)  14.4 us
    all_to_all x2, waiting for transfers between devices, to_tokens(): return lax.all_to_all(panel, BLK, split_axis=0, concat_axis=1, tiled=True)  12.6 us
    dot_general x1, matrix products, shards(): jnp.einsum('tsc,csr->trc', grad_pre_tok, up_mix, preferred_element_type=flt)  9.86 us
  transfers between devices with their start and end apart: 5, of which 4 were waited for; matrix products, arithmetic and copies ran while one was open for 14% of the time, Pallas kernels for 0%

profile of v2, /device:TPU:7, one launch (start us, length us, event | category | flops | bytes accessed | tf_op | source)
XLA Modules:
  0.0 259.5 jit_solution(14811438788652961009)
XLA Ops:
  0.6 0.0 copy-start
  0.6 1.2 copy.63
  1.9 0.0 copy-done
  1.9 0.0 copy-start.3
  1.9 0.5 fusion.29
  2.4 0.0 copy-start.1
  2.4 1.7 copy.64
  4.1 7.8 %all-to-all-start.2 = ((bf16[288,8,256]{2,1,0:T(8,128)(2,1)}), bf16[288,8,256]{2,1,0:T(8,128)(2,1)S(1)}, u32[]{:S(2)}, u32[]{:S(2)}) async-start(bf16[288,8,256]{2,1,0:T(8,128)(2,1)} %copy.64), calls=%async_computation.2 | async-start | bytes 2359296 | tf_op jit(solution)/shard_map/all_to_all | solution.py:23
  12.0 0.0 copy-done.3
  12.0 0.2 copy.54
  12.2 0.0 copy-done.1
  12.2 0.5 fusion.28
  12.7 1.7 copy.55
  14.4 12.6 %all-to-all-done.2 = bf16[288,8,256]{2,1,0:T(8,128)(2,1)S(1)} async-done(((bf16[288,8,256]{2,1,0:T(8,128)(2,1)}), bf16[288,8,256]{2,1,0:T(8,128)(2,1)S(1)}, u32[]{:S(2)}, u32[]{:S(2)}) %all-to-all-start.2) | async-done | bytes 1179680 | tf_op jit(solution)/shard_map/all_to_all | solution.py:23
  27.0 8.2 %all-to-all-start = ((bf16[288,8,256]{2,1,0:T(8,128)(2,1)}), bf16[288,8,256]{2,1,0:T(8,128)(2,1)S(1)}, u32[]{:S(2)}, u32[]{:S(2)}) async-start(bf16[288,8,256]{2,1,0:T(8,128)(2,1)} %copy.55), calls=%async_computation | async-start | bytes 2359296 | tf_op jit(solution)/shard_map/all_to_all | solution.py:23
  35.2 8.4 %copy.58 = bf16[256,96,96]{2,1,0:T(8,128)(2,1)} copy(bf16[256,96,96]{0,2,1:T(8,128)(2,1)} %param.8) | data formatting | bytes 9437184 | tf_op args[2]
  43.6 8.5 %copy.59 = bf16[256,96,96]{2,1,0:T(8,128)(2,1)} copy(bf16[256,96,96]{0,2,1:T(8,128)(2,1)} %param.9) | data formatting | bytes 9437184 | tf_op args[3]
  52.1 1.2 copy.78
  53.3 2.7 %copy.66 = bf16[24,96,256]{1,0,2:T(8,128)(2,1)} copy(bf16[24,96,256]{2,1,0:T(8,128)(2,1)} %bitcast.99) | data formatting | bytes 2359296 | tf_op jit(solution)/shard_map/all_to_all | solution.py:23
  56.0 0.0 all-to-all-done
  56.0 1.2 copy.79
  57.1 1.9 copy.57
  59.1 7.3 %convolution_convert_fusion.3 = bf16[256,24,96]{2,1,0:T(8,128)(2,1)} fusion(bf16[24,96,256]{1,0,2:T(8,128)(2,1)S(1)} %copy.57, bf16[256,96,96]{2,1,0:T(8,128)(2,1)} %copy.58), kind=kOutput, calls=%fused_computation.17 | convolution fusion | flops 113836032 | bytes 7077888 | tf_op jit(solution)/shard_map/trc,csr->tsc/dot_general | solution.py:43
  66.4 9.9 %fusion.25 = bf16[24,96,256]{1,0,2:T(8,128)(2,1)S(1)} fusion(bf16[256,96,96]{2,1,0:T(8,128)(2,1)} %copy.58, bf16[256,24,96]{2,1,0:T(8,128)(2,1)} %convolution_convert_fusion.3, bf16[24,96,256]{1,0,2:T(8,128)(2,1)} %copy.66, bf16[256,96,96]{2,1,0:T(8,128)(2,1)} %copy.59), kind=kOutput, calls=%fused_computation.30 | convolution fusion | flops 240058368 | bytes 12976128 | tf_op jit(solution)/shard_map/tsc,csr->trc/dot_general | solution.py:57
  76.2 2.1 copy.69
  78.4 6.1 %all-to-all-start.3 = ((bf16[24,96,256]{2,0,1:T(8,128)(2,1)}), bf16[24,96,256]{2,0,1:T(8,128)(2,1)S(1)}, u32[]{:S(2)}, u32[]{:S(2)}) async-start(bf16[24,96,256]{2,0,1:T(8,128)(2,1)} %copy.69), calls=%async_computation.3 | async-start | bytes 2359296 | tf_op jit(solution)/shard_map/all_to_all | solution.py:27
  84.4 7.8 %fusion.22 = bf16[24,96,256]{1,0,2:T(8,128)(2,1)} fusion(bf16[256,96,96]{2,1,0:T(8,128)(2,1)} %copy.59, bf16[256,24,96]{2,1,0:T(8,128)(2,1)} %convolution_convert_fusion.3), kind=kOutput, calls=%fused_computation.29 | convolution fusion | flops 119734272 | bytes 7077888 | tf_op jit(solution)/shard_map/tsc,cqs->tqc/dot_general | solution.py:46
  92.2 3.2 %copy.60 = bf16[24,96,256]{2,0,1:T(8,128)(2,1)} copy(bf16[24,96,256]{1,0,2:T(8,128)(2,1)} %fusion.22) | data formatting | bytes 2359296 | tf_op jit(solution)/shard_map/convert_element_type | solution.py:46
  95.4 5.9 %all-to-all-done.3 = bf16[24,96,256]{2,0,1:T(8,128)(2,1)S(1)} async-done(((bf16[24,96,256]{2,0,1:T(8,128)(2,1)}), bf16[24,96,256]{2,0,1:T(8,128)(2,1)S(1)}, u32[]{:S(2)}, u32[]{:S(2)}) %all-to-all-start.3) | async-done | bytes 1179680 | tf_op jit(solution)/shard_map/all_to_all | solution.py:27
  101.3 8.4 %all-to-all-start.1 = ((bf16[24,96,256]{2,0,1:T(8,128)(2,1)}), bf16[24,96,256]{2,0,1:T(8,128)(2,1)}, u32[]{:S(2)}, u32[]{:S(2)}) async-start(bf16[24,96,256]{2,0,1:T(8,128)(2,1)} %copy.60), calls=%async_computation.1 | async-start | bytes 2359296 | tf_op jit(solution)/shard_map/all_to_all | solution.py:27
  109.7 0.1 copy.71
  109.8 18.3 %all-to-all-done.1 = bf16[24,96,256]{2,0,1:T(8,128)(2,1)} async-done(((bf16[24,96,256]{2,0,1:T(8,128)(2,1)}), bf16[24,96,256]{2,0,1:T(8,128)(2,1)}, u32[]{:S(2)}, u32[]{:S(2)}) %all-to-all-start.1) | async-done | bytes 1179680 | tf_op jit(solution)/shard_map/all_to_all | solution.py:27
  128.1 1.4 copy.62
  129.5 0.4 fusion.41
  129.9 0.4 fusion.40
  130.2 0.1 pad_maximum_fusion
  130.3 75.7 %all_to_all.82 = f32[64,16,256]{2,1,0:T(8,128)} all-to-all(f32[64,16,256]{2,1,0:T(8,128)S(1)} %bitcast.101), channel_id=1, replica_groups=mesh['y'=8,'zh'=4,'core'=2,'zl'=3,'x'=4] {'y','zh','core'}, dimensions={0} | all-to-all | bytes 2097152 | tf_op jit(solution)/shard_map/all_to_all | solution.py:67
  206.0 0.0 copy-start.2
  206.0 1.4 reduce_sum.9
  207.4 1.1 broadcast_in_dim.2
  208.5 6.6 %all-to-all-start.5 = ((f32[64,16,256]{2,1,0:T(8,128)}), f32[64,16,256]{2,1,0:T(8,128)}, u32[]{:S(2)}, u32[]{:S(2)}) async-start(f32[64,16,256]{2,1,0:T(8,128)} %broadcast_in_dim.2), calls=%async_computation.5 | async-start | bytes 2097152 | tf_op jit(solution)/shard_map/all_to_all | solution.py:70
  215.1 0.5 convolution_convert_fusion.7
  215.6 0.9 copy.72
  216.5 0.0 copy-done.2
  216.5 0.5 convolution_convert_fusion.6
  217.0 0.9 copy.73
  217.9 39.4 %all-to-all-done.5 = f32[64,16,256]{2,1,0:T(8,128)} async-done(((f32[64,16,256]{2,1,0:T(8,128)}), f32[64,16,256]{2,1,0:T(8,128)}, u32[]{:S(2)}, u32[]{:S(2)}) %all-to-all-start.5) | async-done | bytes 1048608 | tf_op jit(solution)/shard_map/all_to_all | solution.py:70
  257.3 2.2 fusion.39
Async XLA Ops:
  0.6 1.2 copy-start
  1.9 10.1 %copy-start.3 = (bf16[288,512]{1,0:T(8,128)(2,1)S(1)}, bf16[288,512]{1,0:T(8,128)(2,1)}, u32[]{:S(2)}) copy-start(bf16[288,512]{1,0:T(8,128)(2,1)} %param.6) | copy-start | bytes 884740
  2.4 9.8 %copy-start.1 = (bf16[8,64,256]{2,1,0:T(8,128)(2,1)S(1)}, bf16[8,64,256]{2,1,0:T(8,128)(2,1)}, u32[]{:S(2)}) copy-start(bf16[8,64,256]{2,1,0:T(8,128)(2,1)} %param.7) | copy-start | bytes 786436
  4.1 22.9 %all-to-all-start.2 = ((bf16[288,8,256]{2,1,0:T(8,128)(2,1)}), bf16[288,8,256]{2,1,0:T(8,128)(2,1)S(1)}, u32[]{:S(2)}, u32[]{:S(2)}) async-start(bf16[288,8,256]{2,1,0:T(8,128)(2,1)} %copy.64), calls=%async_computation.2 | async-start | bytes 2359296 | tf_op jit(solution)/shard_map/all_to_all | solution.py:23
  27.0 29.0 %all-to-all-start = ((bf16[288,8,256]{2,1,0:T(8,128)(2,1)}), bf16[288,8,256]{2,1,0:T(8,128)(2,1)S(1)}, u32[]{:S(2)}, u32[]{:S(2)}) async-start(bf16[288,8,256]{2,1,0:T(8,128)(2,1)} %copy.55), calls=%async_computation | async-start | bytes 2359296 | tf_op jit(solution)/shard_map/all_to_all | solution.py:23
  78.4 22.9 %all-to-all-start.3 = ((bf16[24,96,256]{2,0,1:T(8,128)(2,1)}), bf16[24,96,256]{2,0,1:T(8,128)(2,1)S(1)}, u32[]{:S(2)}, u32[]{:S(2)}) async-start(bf16[24,96,256]{2,0,1:T(8,128)(2,1)} %copy.69), calls=%async_computation.3 | async-start | bytes 2359296 | tf_op jit(solution)/shard_map/all_to_all | solution.py:27
  101.3 26.8 %all-to-all-start.1 = ((bf16[24,96,256]{2,0,1:T(8,128)(2,1)}), bf16[24,96,256]{2,0,1:T(8,128)(2,1)}, u32[]{:S(2)}, u32[]{:S(2)}) async-start(bf16[24,96,256]{2,0,1:T(8,128)(2,1)} %copy.60), calls=%async_computation.1 | async-start | bytes 2359296 | tf_op jit(solution)/shard_map/all_to_all | solution.py:27
  206.0 10.5 %copy-start.2 = (bf16[8,64,256]{2,1,0:T(8,128)(2,1)S(1)}, bf16[8,64,256]{2,1,0:T(8,128)(2,1)}, u32[]{:S(2)}) copy-start(bf16[8,64,256]{2,1,0:T(8,128)(2,1)} %param.7) | copy-start | bytes 786436
  208.5 48.8 %all-to-all-start.5 = ((f32[64,16,256]{2,1,0:T(8,128)}), f32[64,16,256]{2,1,0:T(8,128)}, u32[]{:S(2)}, u32[]{:S(2)}) async-start(f32[64,16,256]{2,1,0:T(8,128)} %broadcast_in_dim.2), calls=%async_computation.5 | async-start | bytes 2097152 | tf_op jit(solution)/shard_map/all_to_all | solution.py:70

commit v3 on v1

--- a/solution.py
+++ b/solution.py
@@ -4,6 +4,7 @@
 from jax.sharding import PartitionSpec as P, Mesh
 DP = ("y", "zh", "core")
 BLK = ("zl", "x")
+DP_ORDER = ("core", "y", "zh")
 
 gelu_coef = 0.7978845608028654
 cubic_coef = 0.044715
@@ -27,7 +28,21 @@
     return lax.all_to_all(panel, BLK, split_axis=1, concat_axis=0, tiled=True)
 
 
+def dp_sum(total, sizes):
+    lanes = total.shape[-1]
+    for axis in DP_ORDER:
+        count = sizes[axis]
+        pieces = lax.all_to_all(total.reshape(count, -1, lanes), axis, 0, 0, tiled=True)
+        total = pieces.sum(axis=0)
+    for axis in reversed(DP_ORDER):
+        count = sizes[axis]
+        spread = jnp.broadcast_to(total[None], (count,) + total.shape)
+        total = lax.all_to_all(spread, axis, 0, 0, tiled=True).reshape(-1, lanes)
+    return total
+
+
 def shards(tokens, up_first, up_mix, down_mix, down_last, cotangent):
+    mesh_sizes = {"core": 2, "y": 8, "zh": 4}
     flt = jnp.float32
     half = jnp.bfloat16
     row_count = tokens.shape[0]
@@ -64,8 +79,7 @@
     grad_firstw = jnp.einsum("trk,trc->rkc", inputs, grad_first, preferred_element_type=flt)
 
     both = jnp.concatenate([grad_firstw.reshape(-1, grad_firstw.shape[-1]), grad_last.reshape(-1, grad_last.shape[-1])], axis=0)
-    both = lax.psum_scatter(both, DP, scatter_dimension=0, tiled=True)
-    both = lax.all_gather(both, DP, axis=0, tiled=True)
+    both = dp_sum(both, mesh_sizes)
     summed_first, summed_last = jnp.split(both, 2, axis=0)
     summed_first = summed_first.reshape(grad_firstw.shape)
     summed_last = summed_last.reshape(grad_last.shape)

time: 415 us -> 234 us (0.56)
  waiting for transfers between devices: 300 us -> 45 us
  blocking collectives: 0 us -> 82.9 us
  between operations: 14.2 us -> 0.81 us
    reduce_scatter x1 -> x0, waiting for transfers between devices: 171 us -> none  [shards(): both = lax.psum_scatter(both, DP, scatter_dimension=0, tiled=True)]
    all_gather x1 -> x0, waiting for transfers between devices: 92.5 us -> none  [shards(): both = lax.all_gather(both, DP, axis=0, tiled=True)]
    all_to_all x0 -> x5, blocking collectives: none -> 82.9 us  [the longest x3 60.5 us: dp_sum(): lax.all_to_all(total.reshape(count, -1, lanes), axis, 0, 0, tiled=True)]
    all_to_all x0 -> x1, waiting for transfers between devices: none -> 8.17 us  [dp_sum(): total = lax.all_to_all(spread, axis, 0, 0, tiled=True).reshape(-1, lanes)]
    unnamed x14 -> x12, local copies, waits for them, and re-layouts: 20.2 us -> 20 us
  transfers between devices with their start and end apart: 6 -> 5, of which waited for: 5 -> 4; matrix products, arithmetic and copies ran while one was open for 9% -> 16% of each run, Pallas kernels for 0% -> 0%
where the time goes in v3:
time: 234 us; the launch traced here: 233 us
  blocking collectives  82.9 us (35%)
  waiting for transfers between devices  45 us (19%)
  local copies, waits for them, and re-layouts  39 us (17%)
  starting transfers between devices  34 us (15%)
  matrix products  28.7 us (12%)
  other arithmetic  2.51 us (1%)
    all_to_all x3, blocking collectives, dp_sum(): lax.all_to_all(total.reshape(count, -1, lanes), axis, 0, 0, tiled=True)  60.5 us
    all_to_all x2, waiting for transfers between devices, to_blocks(): return lax.all_to_all(panel, BLK, split_axis=1, concat_axis=0, tiled=True)  24.2 us
    all_to_all x2, blocking collectives, dp_sum(): total = lax.all_to_all(spread, axis, 0, 0, tiled=True).reshape(-1, lanes)  22.4 us
    unnamed x12, local copies, waits for them, and re-layouts  20 us
    all_to_all x2, starting transfers between devices, to_tokens(): return lax.all_to_all(panel, BLK, split_axis=0, concat_axis=1, tiled=True)  16.1 us
    all_to_all x2, starting transfers between devices, to_blocks(): return lax.all_to_all(panel, BLK, split_axis=1, concat_axis=0, tiled=True)  14.4 us
    all_to_all x2, waiting for transfers between devices, to_tokens(): return lax.all_to_all(panel, BLK, split_axis=0, concat_axis=1, tiled=True)  12.6 us
    dot_general x1, matrix products, shards(): jnp.einsum('tsc,csr->trc', grad_pre_tok, up_mix, preferred_element_type=flt)  9.86 us
  transfers between devices with their start and end apart: 5, of which 4 were waited for; matrix products, arithmetic and copies ran while one was open for 16% of the time, Pallas kernels for 0%

profile of v3, /device:TPU:7, one launch (start us, length us, event | category | flops | bytes accessed | tf_op | source)
XLA Modules:
  0.0 232.9 jit_solution(1569822440810574420)
XLA Ops:
  0.6 0.0 copy-start
  0.6 1.2 copy.83
  1.9 0.0 copy-start.2
  1.9 0.5 fusion.29
  2.4 0.0 copy-start.1
  2.4 1.7 copy.84
  4.1 7.8 %all-to-all-start.2 = ((bf16[288,8,256]{2,1,0:T(8,128)(2,1)}), bf16[288,8,256]{2,1,0:T(8,128)(2,1)S(1)}, u32[]{:S(2)}, u32[]{:S(2)}) async-start(bf16[288,8,256]{2,1,0:T(8,128)(2,1)} %copy.84), calls=%async_computation.2 | async-start | bytes 2359296 | tf_op jit(solution)/shard_map/all_to_all | solution.py:24
  11.9 0.2 copy.74
  12.2 0.5 fusion.28
  12.7 1.7 copy.75
  14.4 12.6 %all-to-all-done.2 = bf16[288,8,256]{2,1,0:T(8,128)(2,1)S(1)} async-done(((bf16[288,8,256]{2,1,0:T(8,128)(2,1)}), bf16[288,8,256]{2,1,0:T(8,128)(2,1)S(1)}, u32[]{:S(2)}, u32[]{:S(2)}) %all-to-all-start.2) | async-done | bytes 1179680 | tf_op jit(solution)/shard_map/all_to_all | solution.py:24
  26.9 8.2 %all-to-all-start = ((bf16[288,8,256]{2,1,0:T(8,128)(2,1)}), bf16[288,8,256]{2,1,0:T(8,128)(2,1)S(1)}, u32[]{:S(2)}, u32[]{:S(2)}) async-start(bf16[288,8,256]{2,1,0:T(8,128)(2,1)} %copy.75), calls=%async_computation | async-start | bytes 2359296 | tf_op jit(solution)/shard_map/all_to_all | solution.py:24
  35.2 8.4 %copy.78 = bf16[256,96,96]{2,1,0:T(8,128)(2,1)} copy(bf16[256,96,96]{0,2,1:T(8,128)(2,1)} %param.8) | data formatting | bytes 9437184 | tf_op args[2]
  43.6 8.4 %copy.79 = bf16[256,96,96]{2,1,0:T(8,128)(2,1)} copy(bf16[256,96,96]{0,2,1:T(8,128)(2,1)} %param.9) | data formatting | bytes 9437184 | tf_op args[3]
  52.0 1.2 copy.98
  53.2 2.7 %copy.86 = bf16[24,96,256]{1,0,2:T(8,128)(2,1)} copy(bf16[24,96,256]{2,1,0:T(8,128)(2,1)} %bitcast.103) | data formatting | bytes 2359296 | tf_op jit(solution)/shard_map/all_to_all | solution.py:24
  55.8 1.2 copy.99
  57.0 1.9 copy.77
  58.9 7.3 %convolution_convert_fusion.3 = bf16[256,24,96]{2,1,0:T(8,128)(2,1)} fusion(bf16[24,96,256]{1,0,2:T(8,128)(2,1)S(1)} %copy.77, bf16[256,96,96]{2,1,0:T(8,128)(2,1)} %copy.78), kind=kOutput, calls=%fused_computation.17 | convolution fusion | flops 113836032 | bytes 7077888 | tf_op jit(solution)/shard_map/trc,csr->tsc/dot_general | solution.py:58
  66.2 9.9 %fusion.25 = bf16[24,96,256]{1,0,2:T(8,128)(2,1)S(1)} fusion(bf16[256,96,96]{2,1,0:T(8,128)(2,1)} %copy.78, bf16[256,24,96]{2,1,0:T(8,128)(2,1)} %convolution_convert_fusion.3, bf16[24,96,256]{1,0,2:T(8,128)(2,1)} %copy.86, bf16[256,96,96]{2,1,0:T(8,128)(2,1)} %copy.79), kind=kOutput, calls=%fused_computation.30 | convolution fusion | flops 240058368 | bytes 12976128 | tf_op jit(solution)/shard_map/tsc,csr->trc/dot_general | solution.py:72
  76.1 2.2 copy.89
  78.3 6.1 %all-to-all-start.3 = ((bf16[24,96,256]{2,0,1:T(8,128)(2,1)}), bf16[24,96,256]{2,0,1:T(8,128)(2,1)S(1)}, u32[]{:S(2)}, u32[]{:S(2)}) async-start(bf16[24,96,256]{2,0,1:T(8,128)(2,1)} %copy.89), calls=%async_computation.3 | async-start | bytes 2359296 | tf_op jit(solution)/shard_map/all_to_all | solution.py:28
  84.3 7.8 %fusion.22 = bf16[24,96,256]{1,0,2:T(8,128)(2,1)} fusion(bf16[256,96,96]{2,1,0:T(8,128)(2,1)} %copy.79, bf16[256,24,96]{2,1,0:T(8,128)(2,1)} %convolution_convert_fusion.3), kind=kOutput, calls=%fused_computation.29 | convolution fusion | flops 119734272 | bytes 7077888 | tf_op jit(solution)/shard_map/tsc,cqs->tqc/dot_general | solution.py:61
  92.1 3.2 %copy.80 = bf16[24,96,256]{2,0,1:T(8,128)(2,1)} copy(bf16[24,96,256]{1,0,2:T(8,128)(2,1)} %fusion.22) | data formatting | bytes 2359296 | tf_op jit(solution)/shard_map/convert_element_type | solution.py:61
  95.3 5.9 %all-to-all-done.3 = bf16[24,96,256]{2,0,1:T(8,128)(2,1)S(1)} async-done(((bf16[24,96,256]{2,0,1:T(8,128)(2,1)}), bf16[24,96,256]{2,0,1:T(8,128)(2,1)S(1)}, u32[]{:S(2)}, u32[]{:S(2)}) %all-to-all-start.3) | async-done | bytes 1179680 | tf_op jit(solution)/shard_map/all_to_all | solution.py:28
  101.2 8.4 %all-to-all-start.1 = ((bf16[24,96,256]{2,0,1:T(8,128)(2,1)}), bf16[24,96,256]{2,0,1:T(8,128)(2,1)}, u32[]{:S(2)}, u32[]{:S(2)}) async-start(bf16[24,96,256]{2,0,1:T(8,128)(2,1)} %copy.80), calls=%async_computation.1 | async-start | bytes 2359296 | tf_op jit(solution)/shard_map/all_to_all | solution.py:28
  109.5 0.1 copy.91
  109.6 18.4 %all-to-all-done.1 = bf16[24,96,256]{2,0,1:T(8,128)(2,1)} async-done(((bf16[24,96,256]{2,0,1:T(8,128)(2,1)}), bf16[24,96,256]{2,0,1:T(8,128)(2,1)}, u32[]{:S(2)}, u32[]{:S(2)}) %all-to-all-start.1) | async-done | bytes 1179680 | tf_op jit(solution)/shard_map/all_to_all | solution.py:28
  128.0 1.4 copy.82
  129.4 0.4 fusion.41
  129.7 0.4 fusion.40
  130.1 0.1 pad_maximum_fusion
  130.2 8.4 %all_to_all.102 = f32[2,512,256]{2,1,0:T(8,128)} all-to-all(f32[2,512,256]{2,1,0:T(8,128)S(1)} %bitcast.105), channel_id=1, replica_groups=mesh['y'=8,'zh'=4,'core'=2,'zl'=3,'x'=4] {'core'}, dimensions={0} | all-to-all | bytes 2097152 | tf_op jit(solution)/shard_map/all_to_all | solution.py:35
  138.6 1.4 reduce_sum.27
  140.0 25.2 %all_to_all.103 = f32[8,64,256]{2,1,0:T(8,128)} all-to-all(f32[8,64,256]{2,1,0:T(8,128)S(1)} %bitcast.111), channel_id=1, replica_groups=mesh['y'=8,'zh'=4,'core'=2,'zl'=3,'x'=4] {'y'}, dimensions={0} | all-to-all | bytes 1048576 | tf_op jit(solution)/shard_map/all_to_all | solution.py:35
  165.2 1.1 reduce_sum.28
  166.3 26.9 %all_to_all.104 = f32[4,16,256]{2,1,0:T(8,128)S(1)} all-to-all(f32[4,16,256]{2,1,0:T(8,128)S(1)} %bitcast.119), channel_id=1, replica_groups=mesh['y'=8,'zh'=4,'core'=2,'zl'=3,'x'=4] {'zh'}, dimensions={0} | all-to-all | bytes 131072 | tf_op jit(solution)/shard_map/all_to_all | solution.py:35
  193.2 11.7 %all_to_all.105 = f32[4,16,256]{2,1,0:T(8,128)S(1)} all-to-all(f32[4,16,256]{2,1,0:T(8,128)S(1)} %broadcast_in_dim.20), channel_id=1, replica_groups=mesh['y'=8,'zh'=4,'core'=2,'zl'=3,'x'=4] {'zh'}, dimensions={0} | all-to-all | bytes 131072 | tf_op jit(solution)/shard_map/all_to_all | solution.py:40
  204.9 0.8 broadcast_in_dim.22
  205.7 3.5 %all-to-all-start.8 = ((f32[8,64,256]{2,1,0:T(8,128)}), f32[8,64,256]{2,1,0:T(8,128)S(1)}, u32[]{:S(2)}, u32[]{:S(2)}) async-start(f32[8,64,256]{2,1,0:T(8,128)} %broadcast_in_dim.22), calls=%async_computation.8 | async-start | bytes 1048576 | tf_op jit(solution)/shard_map/all_to_all | solution.py:40
  209.2 0.5 convolution_convert_fusion.7
  209.7 0.9 copy.92
  210.6 1.4 convolution_convert_fusion.6
  212.0 0.9 copy.93
  212.9 8.2 %all-to-all-done.8 = f32[8,64,256]{2,1,0:T(8,128)S(1)} async-done(((f32[8,64,256]{2,1,0:T(8,128)}), f32[8,64,256]{2,1,0:T(8,128)S(1)}, u32[]{:S(2)}, u32[]{:S(2)}) %all-to-all-start.8) | async-done | bytes 524320 | tf_op jit(solution)/shard_map/all_to_all | solution.py:40
  221.1 0.1 broadcast_in_dim.24
  221.2 10.7 %all_to_all.106 = f32[2,512,256]{2,1,0:T(8,128)S(1)} all-to-all(f32[2,512,256]{2,1,0:T(8,128)S(1)} %broadcast_in_dim.24), channel_id=1, replica_groups=mesh['y'=8,'zh'=4,'core'=2,'zl'=3,'x'=4] {'core'}, dimensions={0} | all-to-all | bytes 2097152 | tf_op jit(solution)/shard_map/all_to_all | solution.py:40
  231.9 1.0 fusion.39
  (6 shorter events, 0.0 us)
Async XLA Ops:
  0.6 1.2 copy-start
  1.9 10.1 %copy-start.2 = (bf16[288,512]{1,0:T(8,128)(2,1)S(1)}, bf16[288,512]{1,0:T(8,128)(2,1)}, u32[]{:S(2)}) copy-start(bf16[288,512]{1,0:T(8,128)(2,1)} %param.6) | copy-start | bytes 884740
  2.4 9.8 %copy-start.1 = (bf16[8,64,256]{2,1,0:T(8,128)(2,1)S(1)}, bf16[8,64,256]{2,1,0:T(8,128)(2,1)}, u32[]{:S(2)}) copy-start(bf16[8,64,256]{2,1,0:T(8,128)(2,1)} %param.7) | copy-start | bytes 786436
  4.1 22.9 %all-to-all-start.2 = ((bf16[288,8,256]{2,1,0:T(8,128)(2,1)}), bf16[288,8,256]{2,1,0:T(8,128)(2,1)S(1)}, u32[]{:S(2)}, u32[]{:S(2)}) async-start(bf16[288,8,256]{2,1,0:T(8,128)(2,1)} %copy.84), calls=%async_computation.2 | async-start | bytes 2359296 | tf_op jit(solution)/shard_map/all_to_all | solution.py:24
  26.9 28.9 %all-to-all-start = ((bf16[288,8,256]{2,1,0:T(8,128)(2,1)}), bf16[288,8,256]{2,1,0:T(8,128)(2,1)S(1)}, u32[]{:S(2)}, u32[]{:S(2)}) async-start(bf16[288,8,256]{2,1,0:T(8,128)(2,1)} %copy.75), calls=%async_computation | async-start | bytes 2359296 | tf_op jit(solution)/shard_map/all_to_all | solution.py:24
  78.3 22.9 %all-to-all-start.3 = ((bf16[24,96,256]{2,0,1:T(8,128)(2,1)}), bf16[24,96,256]{2,0,1:T(8,128)(2,1)S(1)}, u32[]{:S(2)}, u32[]{:S(2)}) async-start(bf16[24,96,256]{2,0,1:T(8,128)(2,1)} %copy.89), calls=%async_computation.3 | async-start | bytes 2359296 | tf_op jit(solution)/shard_map/all_to_all | solution.py:28
  101.2 26.8 %all-to-all-start.1 = ((bf16[24,96,256]{2,0,1:T(8,128)(2,1)}), bf16[24,96,256]{2,0,1:T(8,128)(2,1)}, u32[]{:S(2)}, u32[]{:S(2)}) async-start(bf16[24,96,256]{2,0,1:T(8,128)(2,1)} %copy.80), calls=%async_computation.1 | async-start | bytes 2359296 | tf_op jit(solution)/shard_map/all_to_all | solution.py:28
  205.7 15.4 %all-to-all-start.8 = ((f32[8,64,256]{2,1,0:T(8,128)}), f32[8,64,256]{2,1,0:T(8,128)S(1)}, u32[]{:S(2)}, u32[]{:S(2)}) async-start(f32[8,64,256]{2,1,0:T(8,128)} %broadcast_in_dim.22), calls=%async_computation.8 | async-start | bytes 1048576 | tf_op jit(solution)/shard_map/all_to_all | solution.py:40

commit v4 on v3

--- a/solution.py
+++ b/solution.py
@@ -21,11 +21,11 @@
 
 
 def to_tokens(panel):
-    return lax.all_to_all(panel, BLK, split_axis=0, concat_axis=1, tiled=True)
+    return lax.all_to_all(panel, BLK, split_axis=1, concat_axis=2, tiled=True)
 
 
 def to_blocks(panel):
-    return lax.all_to_all(panel, BLK, split_axis=1, concat_axis=0, tiled=True)
+    return lax.all_to_all(panel, BLK, split_axis=2, concat_axis=1, tiled=True)
 
 
 def dp_sum(total, sizes):
@@ -54,17 +54,13 @@
     grad_mixed = jnp.einsum("tqk,qkc->tqc", outgrads, down_last, preferred_element_type=flt).astype(
         half
     )
-    first_tok = to_tokens(first)
+    first_tok, grad_mixed_tok = to_tokens(jnp.stack([first, grad_mixed]))
     pre_tok = jnp.einsum("trc,csr->tsc", first_tok, up_mix, preferred_element_type=flt).astype(half)
     hidden_f, slope = gelu_pair(pre_tok.astype(flt))
     hidden_tok = hidden_f.astype(half)
     mixed_tok = jnp.einsum("tsc,cqs->tqc", hidden_tok, down_mix, preferred_element_type=flt).astype(
         half
     )
-    mixed = to_blocks(mixed_tok)
-    encoded = jnp.einsum("tqc,qkc->tqk", mixed, down_last, preferred_element_type=flt).astype(half)
-    grad_last = jnp.einsum("tqk,tqc->qkc", outgrads, mixed, preferred_element_type=flt)
-    grad_mixed_tok = to_tokens(grad_mixed)
     grad_hidden_tok = jnp.einsum(
         "tqc,cqs->tsc", grad_mixed_tok, down_mix, preferred_element_type=flt
     ).astype(half)
@@ -72,7 +68,9 @@
     grad_first_tok = jnp.einsum(
         "tsc,csr->trc", grad_pre_tok, up_mix, preferred_element_type=flt
     ).astype(half)
-    grad_first = to_blocks(grad_first_tok)
+    mixed, grad_first = to_blocks(jnp.stack([mixed_tok, grad_first_tok]))
+    encoded = jnp.einsum("tqc,qkc->tqk", mixed, down_last, preferred_element_type=flt).astype(half)
+    grad_last = jnp.einsum("tqk,tqc->qkc", outgrads, mixed, preferred_element_type=flt)
     grad_in = jnp.einsum("trc,rkc->trk", grad_first, up_first, preferred_element_type=flt).astype(
         half
     )

time: 234 us -> 232 us (level)
  blocking collectives: 82.9 us -> 124 us
  starting transfers between devices: 34 us -> 11.3 us
  waiting for transfers between devices: 45 us -> 23.1 us
  local copies, waits for them, and re-layouts: 39 us -> 35.9 us
  other arithmetic: 2.51 us -> 5.32 us
    all_to_all x0 -> x1, blocking collectives: none -> 47 us  [to_blocks(): return lax.all_to_all(panel, BLK, split_axis=2, concat_axis=1, tiled=True)]
    all_to_all x4 -> x1, starting transfers between devices: 30.5 us -> 7.83 us  [to_tokens(): return lax.all_to_all(panel, BLK, split_axis=1, concat_axis=2, tiled=True)]
    all_to_all x4 -> x1, waiting for transfers between devices: 36.8 us -> 15 us  [to_tokens(): return lax.all_to_all(panel, BLK, split_axis=1, concat_axis=2, tiled=True)]
    another operation x0 -> x9, local copies, waits for them, and re-layouts: none -> 11.4 us  [the longest x5 6.4 us: shards(): first_tok, grad_mixed_tok = to_tokens(jnp.stack([first, grad_mixed]))]
    convert_element_type x4 -> x0, local copies, waits for them, and re-layouts: 8.71 us -> none  [the longest x1 3.21 us: shards(): jnp.einsum('tsc,cqs->tqc', hidden_tok, down_mix, preferred_element_type=flt)]
    all_to_all x6 -> x2, local copies, waits for them, and re-layouts: 8.35 us -> 1.03 us  [the longest x1 0.87 us: to_blocks(): return lax.all_to_all(panel, BLK, split_axis=2, concat_axis=1, tiled=True)]
    all_to_all x3, blocking collectives: 60.5 us -> 54.9 us  [dp_sum(): lax.all_to_all(total.reshape(count, -1, lanes), axis, 0, 0, tiled=True)]
    another operation x0 -> x2, other arithmetic: none -> 2.81 us  [the longest x1 2.59 us: shards(): mixed, grad_first = to_blocks(jnp.stack([mixed_tok, grad_first_tok]))]
  transfers between devices with their start and end apart: 5 -> 2, of which waited for: 4 -> 2; matrix products, arithmetic and copies ran while one was open for 16% -> 9% of each run, Pallas kernels for 0% -> 0%
where the time goes in v4:
time: 232 us; the launch traced here: 229 us
  blocking collectives  124 us (53%)
  local copies, waits for them, and re-layouts  35.9 us (15%)
  matrix products  28.6 us (12%)
  waiting for transfers between devices  23.1 us (10%)
  starting transfers between devices  11.3 us (5%)
  other arithmetic  5.32 us (2%)
    all_to_all x3, blocking collectives, dp_sum(): lax.all_to_all(total.reshape(count, -1, lanes), axis, 0, 0, tiled=True)  54.9 us
    all_to_all x1, blocking collectives, to_blocks(): return lax.all_to_all(panel, BLK, split_axis=2, concat_axis=1, tiled=True)  47 us
    all_to_all x2, blocking collectives, dp_sum(): total = lax.all_to_all(spread, axis, 0, 0, tiled=True).reshape(-1, lanes)  22.4 us
    unnamed x18, local copies, waits for them, and re-layouts  21.5 us
    all_to_all x1, waiting for transfers between devices, to_tokens(): return lax.all_to_all(panel, BLK, split_axis=1, concat_axis=2, tiled=True)  15 us
    dot_general x1, matrix products, shards(): jnp.einsum('tsc,csr->trc', grad_pre_tok, up_mix, preferred_element_type=flt)  10.1 us
    all_to_all x1, waiting for transfers between devices, dp_sum(): total = lax.all_to_all(spread, axis, 0, 0, tiled=True).reshape(-1, lanes)  8.11 us
    all_to_all x1, starting transfers between devices, to_tokens(): return lax.all_to_all(panel, BLK, split_axis=1, concat_axis=2, tiled=True)  7.83 us
  transfers between devices with their start and end apart: 2, of which 2 were waited for; matrix products, arithmetic and copies ran while one was open for 9% of the time, Pallas kernels for 0%

profile of v4, /device:TPU:7, one launch (start us, length us, event | category | flops | bytes accessed | tf_op | source)
XLA Modules:
  0.0 229.3 jit_solution(17294827072723299384)
XLA Ops:
  0.6 0.0 copy-start
  0.6 1.2 copy.67
  1.9 0.0 copy-start.3
  1.9 1.3 copy.68
  3.2 1.6 fusion.29
  4.8 0.5 fusion.28
  5.4 0.2 pad_maximum_fusion.1
  5.6 2.8 %copy.69 = bf16[2,288,8,256]{3,2,0,1:T(8,128)(2,1)} copy(bf16[2,288,8,256]{3,1,2,0:T(8,128)(2,1)S(1)} %pad_maximum_fusion.1) | data formatting | bytes 4718592 | tf_op jit(solution)/shard_map/stack | solution.py:57
  8.4 7.8 %all-to-all-start = ((bf16[2,288,8,256]{3,2,0,1:T(8,128)(2,1)}), bf16[2,288,8,256]{3,2,0,1:T(8,128)(2,1)S(1)}, u32[]{:S(2)}, u32[]{:S(2)}) async-start(bf16[2,288,8,256]{3,2,0,1:T(8,128)(2,1)} %copy.69), calls=%async_computation | async-start | bytes 4718592 | tf_op jit(solution)/shard_map/all_to_all | solution.py:24
  16.2 8.4 %copy.73 = bf16[256,96,96]{2,1,0:T(8,128)(2,1)} copy(bf16[256,96,96]{0,2,1:T(8,128)(2,1)} %param.8) | data formatting | bytes 9437184 | tf_op args[2]
  24.6 8.4 %copy.74 = bf16[256,96,96]{2,1,0:T(8,128)(2,1)} copy(bf16[256,96,96]{0,2,1:T(8,128)(2,1)} %param.9) | data formatting | bytes 9437184 | tf_op args[3]
  33.0 15.0 %all-to-all-done = bf16[2,288,8,256]{3,2,0,1:T(8,128)(2,1)S(1)} async-done(((bf16[2,288,8,256]{3,2,0,1:T(8,128)(2,1)}), bf16[2,288,8,256]{3,2,0,1:T(8,128)(2,1)S(1)}, u32[]{:S(2)}, u32[]{:S(2)}) %all-to-all-start) | async-done | bytes 2359328 | tf_op jit(solution)/shard_map/all_to_all | solution.py:24
  48.1 0.2 copy.70
  48.2 0.2 fusion.40
  48.4 0.3 copy_bitcast_fusion.1
  48.7 1.9 copy.76
  50.6 1.3 copy.72
  51.9 6.1 %convolution_convert_fusion.3 = bf16[256,24,96]{2,1,0:T(8,128)(2,1)S(1)} fusion(bf16[24,96,256]{1,0,2:T(8,128)(2,1)S(1)} %copy.72, bf16[256,96,96]{2,1,0:T(8,128)(2,1)} %copy.73), kind=kOutput, calls=%fused_computation.20 | convolution fusion | flops 113836032 | bytes 7077888 | tf_op jit(solution)/shard_map/trc,csr->tsc/dot_general | solution.py:58
  58.0 7.5 %fusion.22 = bf16[1,24,96,256]{2,1,3,0:T(8,128)(2,1)} fusion(bf16[256,96,96]{2,1,0:T(8,128)(2,1)} %copy.74, bf16[256,24,96]{2,1,0:T(8,128)(2,1)S(1)} %convolution_convert_fusion.3), kind=kOutput, calls=%fused_computation.32 | convolution fusion | flops 119734272 | bytes 7077888 | tf_op jit(solution)/shard_map/tsc,cqs->tqc/dot_general | solution.py:61
  65.5 10.1 %fusion.25 = bf16[1,24,96,256]{2,1,3,0:T(8,128)(2,1)} fusion(bf16[256,96,96]{2,1,0:T(8,128)(2,1)} %copy.73, bf16[256,24,96]{2,1,0:T(8,128)(2,1)S(1)} %convolution_convert_fusion.3, bf16[24,96,256]{1,0,2:T(8,128)(2,1)S(1)} %copy-done.5, bf16[256,96,96]{2,1,0:T(8,128)(2,1)} %copy.74), kind=kOutput, calls=%fused_computation.33 | convolution fusion | flops 240058368 | bytes 12976128 | tf_op jit(solution)/shard_map/tsc,csr->trc/dot_general | solution.py:68
  75.6 2.6 %pad_maximum_fusion = bf16[2,24,96,256]{2,1,3,0:T(8,128)(2,1)S(1)} fusion(bf16[1,24,96,256]{2,1,3,0:T(8,128)(2,1)} %fusion.25, bf16[1,24,96,256]{2,1,3,0:T(8,128)(2,1)} %fusion.22), kind=kLoop, calls=%fused_computation.9 | loop fusion | flops 1179648 | bytes 4718592 | tf_op jit(solution)/shard_map/stack | solution.py:71
  78.2 3.6 %copy.79 = bf16[2,24,96,256]{3,1,0,2:T(8,128)(2,1)} copy(bf16[2,24,96,256]{2,1,3,0:T(8,128)(2,1)S(1)} %pad_maximum_fusion) | data formatting | bytes 4718592 | tf_op jit(solution)/shard_map/stack | solution.py:71
  81.8 47.0 %all_to_all.60 = bf16[2,24,96,256]{3,1,0,2:T(8,128)(2,1)S(1)} all-to-all(bf16[2,24,96,256]{3,1,0,2:T(8,128)(2,1)} %copy.79), channel_id=1, replica_groups=mesh['y'=8,'zh'=4,'core'=2,'zl'=3,'x'=4] {'zl','x'}, dimensions={2} | all-to-all | bytes 4718592 | tf_op jit(solution)/shard_map/all_to_all | solution.py:28
  128.7 0.9 copy.88
  129.6 0.2 fusion.39
  129.8 0.0 copy-start.4
  129.8 0.7 copy.82
  130.5 0.3 copy-done.4
  130.8 0.4 fusion.42
  131.2 0.7 copy.81
  131.8 0.4 fusion.43
  132.2 0.1 pad_maximum_fusion.2
  132.3 7.3 %all_to_all.61 = f32[2,512,256]{2,1,0:T(8,128)} all-to-all(f32[2,512,256]{2,1,0:T(8,128)S(1)} %bitcast.104), channel_id=1, replica_groups=mesh['y'=8,'zh'=4,'core'=2,'zl'=3,'x'=4] {'core'}, dimensions={0} | all-to-all | bytes 2097152 | tf_op jit(solution)/shard_map/all_to_all | solution.py:35
  139.6 1.4 reduce_sum.27
  141.0 23.3 %all_to_all.62 = f32[8,64,256]{2,1,0:T(8,128)} all-to-all(f32[8,64,256]{2,1,0:T(8,128)S(1)} %bitcast.110), channel_id=1, replica_groups=mesh['y'=8,'zh'=4,'core'=2,'zl'=3,'x'=4] {'y'}, dimensions={0} | all-to-all | bytes 1048576 | tf_op jit(solution)/shard_map/all_to_all | solution.py:35
  164.3 1.1 reduce_sum.28
  165.4 24.3 %all_to_all.63 = f32[4,16,256]{2,1,0:T(8,128)S(1)} all-to-all(f32[4,16,256]{2,1,0:T(8,128)S(1)} %bitcast.118), channel_id=1, replica_groups=mesh['y'=8,'zh'=4,'core'=2,'zl'=3,'x'=4] {'zh'}, dimensions={0} | all-to-all | bytes 131072 | tf_op jit(solution)/shard_map/all_to_all | solution.py:35
  189.6 11.6 %all_to_all.64 = f32[4,16,256]{2,1,0:T(8,128)S(1)} all-to-all(f32[4,16,256]{2,1,0:T(8,128)S(1)} %broadcast_in_dim.20), channel_id=1, replica_groups=mesh['y'=8,'zh'=4,'core'=2,'zl'=3,'x'=4] {'zh'}, dimensions={0} | all-to-all | bytes 131072 | tf_op jit(solution)/shard_map/all_to_all | solution.py:40
  201.3 0.8 broadcast_in_dim.22
  202.1 3.5 %all-to-all-start.6 = ((f32[8,64,256]{2,1,0:T(8,128)}), f32[8,64,256]{2,1,0:T(8,128)S(1)}, u32[]{:S(2)}, u32[]{:S(2)}) async-start(f32[8,64,256]{2,1,0:T(8,128)} %broadcast_in_dim.22), calls=%async_computation.6 | async-start | bytes 1048576 | tf_op jit(solution)/shard_map/all_to_all | solution.py:40
  205.6 0.5 convolution_convert_fusion.6
  206.1 0.9 copy.84
  207.0 1.4 convolution_convert_fusion.7
  208.4 0.9 copy.83
  209.3 8.1 %all-to-all-done.6 = f32[8,64,256]{2,1,0:T(8,128)S(1)} async-done(((f32[8,64,256]{2,1,0:T(8,128)}), f32[8,64,256]{2,1,0:T(8,128)S(1)}, u32[]{:S(2)}, u32[]{:S(2)}) %all-to-all-start.6) | async-done | bytes 524320 | tf_op jit(solution)/shard_map/all_to_all | solution.py:40
  217.4 0.1 broadcast_in_dim.24
  217.5 10.8 %all_to_all.65 = f32[2,512,256]{2,1,0:T(8,128)S(1)} all-to-all(f32[2,512,256]{2,1,0:T(8,128)S(1)} %broadcast_in_dim.24), channel_id=1, replica_groups=mesh['y'=8,'zh'=4,'core'=2,'zl'=3,'x'=4] {'core'}, dimensions={0} | all-to-all | bytes 2097152 | tf_op jit(solution)/shard_map/all_to_all | solution.py:40
  228.3 1.0 fusion.41
  (10 shorter events, 0.0 us)
Async XLA Ops:
  0.6 4.2 %copy-start = (bf16[8,64,256]{2,1,0:T(8,128)(2,1)S(1)}, bf16[8,64,256]{2,1,0:T(8,128)(2,1)}, u32[]{:S(2)}) copy-start(bf16[8,64,256]{2,1,0:T(8,128)(2,1)} %param.7) | copy-start | bytes 786436
  1.9 3.7 %copy-start.3 = (bf16[288,512]{0,1:T(8,128)(2,1)}, bf16[288,512]{0,1:T(8,128)(2,1)S(1)}, u32[]{:S(2)}) copy-start(bf16[288,512]{0,1:T(8,128)(2,1)S(1)} %copy.67) | copy-start | bytes 884740
  3.2 2.4 %copy-start.1 = (bf16[288,512]{0,1:T(8,128)(2,1)}, bf16[288,512]{0,1:T(8,128)(2,1)S(1)}, u32[]{:S(2)}) copy-start(bf16[288,512]{0,1:T(8,128)(2,1)S(1)} %copy.68) | copy-start | bytes 884740
  8.4 39.7 %all-to-all-start = ((bf16[2,288,8,256]{3,2,0,1:T(8,128)(2,1)}), bf16[2,288,8,256]{3,2,0,1:T(8,128)(2,1)S(1)}, u32[]{:S(2)}, u32[]{:S(2)}) async-start(bf16[2,288,8,256]{3,2,0,1:T(8,128)(2,1)} %copy.69), calls=%async_computation | async-start | bytes 4718592 | tf_op jit(solution)/shard_map/all_to_all | solution.py:24
  58.0 7.5 %copy-start.5 = (bf16[24,96,256]{1,0,2:T(8,128)(2,1)S(1)}, bf16[24,96,256]{1,0,2:T(8,128)(2,1)}, u32[]{:S(2)}) copy-start(bf16[24,96,256]{1,0,2:T(8,128)(2,1)} %copy.76) | copy-start | bytes 3538948
  129.8 1.0 copy-start.4
  130.4 1.4 copy-start.2
  202.1 15.3 %all-to-all-start.6 = ((f32[8,64,256]{2,1,0:T(8,128)}), f32[8,64,256]{2,1,0:T(8,128)S(1)}, u32[]{:S(2)}, u32[]{:S(2)}) async-start(f32[8,64,256]{2,1,0:T(8,128)} %broadcast_in_dim.22), calls=%async_computation.6 | async-start | bytes 1048576 | tf_op jit(solution)/shard_map/all_to_all | solution.py:40

commit v5 on v4

--- a/solution.py
+++ b/solution.py
@@ -30,11 +30,14 @@
 
 def dp_sum(total, sizes):
     lanes = total.shape[-1]
-    for axis in DP_ORDER:
+    for axis in DP_ORDER[:-1]:
         count = sizes[axis]
         pieces = lax.all_to_all(total.reshape(count, -1, lanes), axis, 0, 0, tiled=True)
         total = pieces.sum(axis=0)
-    for axis in reversed(DP_ORDER):
+    count = sizes[DP_ORDER[-1]]
+    spread = jnp.broadcast_to(total[None], (count,) + total.shape)
+    total = lax.all_to_all(spread, DP_ORDER[-1], 0, 0, tiled=True).sum(axis=0)
+    for axis in reversed(DP_ORDER[:-1]):
         count = sizes[axis]
         spread = jnp.broadcast_to(total[None], (count,) + total.shape)
         total = lax.all_to_all(spread, axis, 0, 0, tiled=True).reshape(-1, lanes)

time: 232 us -> 222 us (0.957)
  blocking collectives: 124 us -> 113 us
  waiting for transfers between devices: 23.1 us -> 26.4 us
    all_to_all x0 -> x1, blocking collectives: none -> 27.7 us  [dp_sum(): total = lax.all_to_all(spread, DP_ORDER[-1], 0, 0, tiled=True).sum(axis=0)]
    all_to_all x3 -> x2, blocking collectives: 54.9 us -> 30.6 us  [dp_sum(): lax.all_to_all(total.reshape(count, -1, lanes), axis, 0, 0, tiled=True)]
    all_to_all x2 -> x1, blocking collectives: 22.4 us -> 7.46 us  [dp_sum(): total = lax.all_to_all(spread, axis, 0, 0, tiled=True).reshape(-1, lanes)]
    all_to_all x1, waiting for transfers between devices: 8.11 us -> 11.4 us  [dp_sum(): total = lax.all_to_all(spread, axis, 0, 0, tiled=True).reshape(-1, lanes)]
where the time goes in v5:
time: 222 us; the launch traced here: 221 us
  blocking collectives  113 us (51%)
  local copies, waits for them, and re-layouts  35.9 us (16%)
  matrix products  28.6 us (13%)
  waiting for transfers between devices  26.4 us (12%)
  starting transfers between devices  11.3 us (5%)
  other arithmetic  5.32 us (2%)
    all_to_all x1, blocking collectives, to_blocks(): return lax.all_to_all(panel, BLK, split_axis=2, concat_axis=1, tiled=True)  47 us
    all_to_all x2, blocking collectives, dp_sum(): lax.all_to_all(total.reshape(count, -1, lanes), axis, 0, 0, tiled=True)  30.6 us
    all_to_all x1, blocking collectives, dp_sum(): total = lax.all_to_all(spread, DP_ORDER[-1], 0, 0, tiled=True).sum(axis=0)  27.7 us
    unnamed x18, local copies, waits for them, and re-layouts  21.5 us
    all_to_all x1, waiting for transfers between devices, to_tokens(): return lax.all_to_all(panel, BLK, split_axis=1, concat_axis=2, tiled=True)  15 us
    all_to_all x1, waiting for transfers between devices, dp_sum(): total = lax.all_to_all(spread, axis, 0, 0, tiled=True).reshape(-1, lanes)  11.4 us
    dot_general x1, matrix products, shards(): jnp.einsum('tsc,csr->trc', grad_pre_tok, up_mix, preferred_element_type=flt)  10.1 us
    all_to_all x1, starting transfers between devices, to_tokens(): return lax.all_to_all(panel, BLK, split_axis=1, concat_axis=2, tiled=True)  7.83 us
  transfers between devices with their start and end apart: 2, of which 2 were waited for; matrix products, arithmetic and copies ran while one was open for 9% of the time, Pallas kernels for 0%

profile of v5, /device:TPU:7, one launch (start us, length us, event | category | flops | bytes accessed | tf_op | source)
XLA Modules:
  0.0 221.1 jit_solution(10676993235208804284)
XLA Ops:
  0.6 0.0 copy-start
  0.6 1.2 copy.67
  1.9 1.3 copy.68
  3.2 0.0 copy-start.1
  3.2 1.6 fusion.29
  4.8 0.5 fusion.28
  5.4 0.2 pad_maximum_fusion.1
  5.6 2.8 %copy.69 = bf16[2,288,8,256]{3,2,0,1:T(8,128)(2,1)} copy(bf16[2,288,8,256]{3,1,2,0:T(8,128)(2,1)S(1)} %pad_maximum_fusion.1) | data formatting | bytes 4718592 | tf_op jit(solution)/shard_map/stack | solution.py:60
  8.4 7.8 %all-to-all-start = ((bf16[2,288,8,256]{3,2,0,1:T(8,128)(2,1)}), bf16[2,288,8,256]{3,2,0,1:T(8,128)(2,1)S(1)}, u32[]{:S(2)}, u32[]{:S(2)}) async-start(bf16[2,288,8,256]{3,2,0,1:T(8,128)(2,1)} %copy.69), calls=%async_computation | async-start | bytes 4718592 | tf_op jit(solution)/shard_map/all_to_all | solution.py:24
  16.2 8.4 %copy.73 = bf16[256,96,96]{2,1,0:T(8,128)(2,1)} copy(bf16[256,96,96]{0,2,1:T(8,128)(2,1)} %param.8) | data formatting | bytes 9437184 | tf_op args[2]
  24.6 8.4 %copy.74 = bf16[256,96,96]{2,1,0:T(8,128)(2,1)} copy(bf16[256,96,96]{0,2,1:T(8,128)(2,1)} %param.9) | data formatting | bytes 9437184 | tf_op args[3]
  33.0 15.0 %all-to-all-done = bf16[2,288,8,256]{3,2,0,1:T(8,128)(2,1)S(1)} async-done(((bf16[2,288,8,256]{3,2,0,1:T(8,128)(2,1)}), bf16[2,288,8,256]{3,2,0,1:T(8,128)(2,1)S(1)}, u32[]{:S(2)}, u32[]{:S(2)}) %all-to-all-start) | async-done | bytes 2359328 | tf_op jit(solution)/shard_map/all_to_all | solution.py:24
  48.1 0.2 copy.70
  48.2 0.2 fusion.40
  48.4 0.3 copy_bitcast_fusion.1
  48.7 1.9 copy.76
  50.6 1.3 copy.72
  51.9 6.1 %convolution_convert_fusion.3 = bf16[256,24,96]{2,1,0:T(8,128)(2,1)S(1)} fusion(bf16[24,96,256]{1,0,2:T(8,128)(2,1)S(1)} %copy.72, bf16[256,96,96]{2,1,0:T(8,128)(2,1)} %copy.73), kind=kOutput, calls=%fused_computation.20 | convolution fusion | flops 113836032 | bytes 7077888 | tf_op jit(solution)/shard_map/trc,csr->tsc/dot_general | solution.py:61
  58.0 7.5 %fusion.22 = bf16[1,24,96,256]{2,1,3,0:T(8,128)(2,1)} fusion(bf16[256,96,96]{2,1,0:T(8,128)(2,1)} %copy.74, bf16[256,24,96]{2,1,0:T(8,128)(2,1)S(1)} %convolution_convert_fusion.3), kind=kOutput, calls=%fused_computation.32 | convolution fusion | flops 119734272 | bytes 7077888 | tf_op jit(solution)/shard_map/tsc,cqs->tqc/dot_general | solution.py:64
  65.5 10.1 %fusion.25 = bf16[1,24,96,256]{2,1,3,0:T(8,128)(2,1)} fusion(bf16[256,96,96]{2,1,0:T(8,128)(2,1)} %copy.73, bf16[256,24,96]{2,1,0:T(8,128)(2,1)S(1)} %convolution_convert_fusion.3, bf16[24,96,256]{1,0,2:T(8,128)(2,1)S(1)} %copy-done.5, bf16[256,96,96]{2,1,0:T(8,128)(2,1)} %copy.74), kind=kOutput, calls=%fused_computation.33 | convolution fusion | flops 240058368 | bytes 12976128 | tf_op jit(solution)/shard_map/tsc,csr->trc/dot_general | solution.py:71
  75.6 2.6 %pad_maximum_fusion = bf16[2,24,96,256]{2,1,3,0:T(8,128)(2,1)S(1)} fusion(bf16[1,24,96,256]{2,1,3,0:T(8,128)(2,1)} %fusion.25, bf16[1,24,96,256]{2,1,3,0:T(8,128)(2,1)} %fusion.22), kind=kLoop, calls=%fused_computation.9 | loop fusion | flops 1179648 | bytes 4718592 | tf_op jit(solution)/shard_map/stack | solution.py:74
  78.2 3.6 %copy.79 = bf16[2,24,96,256]{3,1,0,2:T(8,128)(2,1)} copy(bf16[2,24,96,256]{2,1,3,0:T(8,128)(2,1)S(1)} %pad_maximum_fusion) | data formatting | bytes 4718592 | tf_op jit(solution)/shard_map/stack | solution.py:74
  81.8 47.0 %all_to_all.55 = bf16[2,24,96,256]{3,1,0,2:T(8,128)(2,1)S(1)} all-to-all(bf16[2,24,96,256]{3,1,0,2:T(8,128)(2,1)} %copy.79), channel_id=1, replica_groups=mesh['y'=8,'zh'=4,'core'=2,'zl'=3,'x'=4] {'zl','x'}, dimensions={2} | all-to-all | bytes 4718592 | tf_op jit(solution)/shard_map/all_to_all | solution.py:28
  128.7 0.9 copy.88
  129.6 0.2 fusion.39
  129.8 0.0 copy-start.4
  129.8 0.7 copy.82
  130.4 0.0 copy-start.2
  130.5 0.3 copy-done.4
  130.8 0.4 fusion.42
  131.2 0.7 copy.81
  131.8 0.4 fusion.43
  132.2 0.1 pad_maximum_fusion.2
  132.3 7.3 %all_to_all.56 = f32[2,512,256]{2,1,0:T(8,128)} all-to-all(f32[2,512,256]{2,1,0:T(8,128)S(1)} %bitcast.102), channel_id=1, replica_groups=mesh['y'=8,'zh'=4,'core'=2,'zl'=3,'x'=4] {'core'}, dimensions={0} | all-to-all | bytes 2097152 | tf_op jit(solution)/shard_map/all_to_all | solution.py:35
  139.6 1.4 reduce_sum.27
  141.0 23.3 %all_to_all.57 = f32[8,64,256]{2,1,0:T(8,128)} all-to-all(f32[8,64,256]{2,1,0:T(8,128)S(1)} %bitcast.108), channel_id=1, replica_groups=mesh['y'=8,'zh'=4,'core'=2,'zl'=3,'x'=4] {'y'}, dimensions={0} | all-to-all | bytes 1048576 | tf_op jit(solution)/shard_map/all_to_all | solution.py:35
  164.3 1.1 reduce_sum.28
  165.4 27.7 %all_to_all.58 = f32[4,64,256]{2,1,0:T(8,128)S(1)} all-to-all(f32[4,64,256]{2,1,0:T(8,128)S(1)} %broadcast_in_dim.8), channel_id=1, replica_groups=mesh['y'=8,'zh'=4,'core'=2,'zl'=3,'x'=4] {'zh'}, dimensions={0} | all-to-all | bytes 524288 | tf_op jit(solution)/shard_map/all_to_all | solution.py:39
  193.1 0.8 broadcast_in_dim.9
  193.9 3.5 %all-to-all-start.5 = ((f32[8,64,256]{2,1,0:T(8,128)}), f32[8,64,256]{2,1,0:T(8,128)S(1)}, u32[]{:S(2)}, u32[]{:S(2)}) async-start(f32[8,64,256]{2,1,0:T(8,128)} %broadcast_in_dim.9), calls=%async_computation.5 | async-start | bytes 1048576 | tf_op jit(solution)/shard_map/all_to_all | solution.py:43
  197.4 0.5 convolution_convert_fusion.6
  197.9 0.9 copy.84
  198.8 1.4 convolution_convert_fusion.7
  200.2 0.9 copy.83
  201.1 11.4 %all-to-all-done.5 = f32[8,64,256]{2,1,0:T(8,128)S(1)} async-done(((f32[8,64,256]{2,1,0:T(8,128)}), f32[8,64,256]{2,1,0:T(8,128)S(1)}, u32[]{:S(2)}, u32[]{:S(2)}) %all-to-all-start.5) | async-done | bytes 524320 | tf_op jit(solution)/shard_map/all_to_all | solution.py:43
  212.5 0.1 broadcast_in_dim.22
  212.6 7.5 %all_to_all.59 = f32[2,512,256]{2,1,0:T(8,128)S(1)} all-to-all(f32[2,512,256]{2,1,0:T(8,128)S(1)} %broadcast_in_dim.22), channel_id=1, replica_groups=mesh['y'=8,'zh'=4,'core'=2,'zl'=3,'x'=4] {'core'}, dimensions={0} | all-to-all | bytes 2097152 | tf_op jit(solution)/shard_map/all_to_all | solution.py:43
  220.0 1.0 fusion.41
  (9 shorter events, 0.1 us)
Async XLA Ops:
  0.6 4.2 %copy-start = (bf16[8,64,256]{2,1,0:T(8,128)(2,1)S(1)}, bf16[8,64,256]{2,1,0:T(8,128)(2,1)}, u32[]{:S(2)}) copy-start(bf16[8,64,256]{2,1,0:T(8,128)(2,1)} %param.7) | copy-start | bytes 786436
  1.9 3.7 %copy-start.3 = (bf16[288,512]{0,1:T(8,128)(2,1)}, bf16[288,512]{0,1:T(8,128)(2,1)S(1)}, u32[]{:S(2)}) copy-start(bf16[288,512]{0,1:T(8,128)(2,1)S(1)} %copy.67) | copy-start | bytes 884740
  3.2 2.4 %copy-start.1 = (bf16[288,512]{0,1:T(8,128)(2,1)}, bf16[288,512]{0,1:T(8,128)(2,1)S(1)}, u32[]{:S(2)}) copy-start(bf16[288,512]{0,1:T(8,128)(2,1)S(1)} %copy.68) | copy-start | bytes 884740
  8.4 39.7 %all-to-all-start = ((bf16[2,288,8,256]{3,2,0,1:T(8,128)(2,1)}), bf16[2,288,8,256]{3,2,0,1:T(8,128)(2,1)S(1)}, u32[]{:S(2)}, u32[]{:S(2)}) async-start(bf16[2,288,8,256]{3,2,0,1:T(8,128)(2,1)} %copy.69), calls=%async_computation | async-start | bytes 4718592 | tf_op jit(solution)/shard_map/all_to_all | solution.py:24
  58.0 7.5 %copy-start.5 = (bf16[24,96,256]{1,0,2:T(8,128)(2,1)S(1)}, bf16[24,96,256]{1,0,2:T(8,128)(2,1)}, u32[]{:S(2)}) copy-start(bf16[24,96,256]{1,0,2:T(8,128)(2,1)} %copy.76) | copy-start | bytes 3538948
  129.8 1.0 copy-start.4
  130.4 1.4 copy-start.2
  193.9 18.6 %all-to-all-start.5 = ((f32[8,64,256]{2,1,0:T(8,128)}), f32[8,64,256]{2,1,0:T(8,128)S(1)}, u32[]{:S(2)}, u32[]{:S(2)}) async-start(f32[8,64,256]{2,1,0:T(8,128)} %broadcast_in_dim.9), calls=%async_computation.5 | async-start | bytes 1048576 | tf_op jit(solution)/shard_map/all_to_all | solution.py:43

commit v6 on v5

--- a/solution.py
+++ b/solution.py
@@ -5,6 +5,7 @@
 DP = ("y", "zh", "core")
 BLK = ("zl", "x")
 DP_ORDER = ("core", "y", "zh")
+CHUNKS = 2
 
 gelu_coef = 0.7978845608028654
 cubic_coef = 0.044715
@@ -44,15 +45,9 @@
     return total
 
 
-def shards(tokens, up_first, up_mix, down_mix, down_last, cotangent):
-    mesh_sizes = {"core": 2, "y": 8, "zh": 4}
+def pipeline(inputs, outgrads, up_first, up_mix, down_mix, down_last):
     flt = jnp.float32
     half = jnp.bfloat16
-    row_count = tokens.shape[0]
-    local_blocks = up_first.shape[0]
-    width_in = up_first.shape[1]
-    inputs = tokens.reshape(row_count, local_blocks, width_in)
-    outgrads = cotangent.reshape(row_count, local_blocks, width_in)
     first = jnp.einsum("trk,rkc->trc", inputs, up_first, preferred_element_type=flt).astype(half)
     grad_mixed = jnp.einsum("tqk,qkc->tqc", outgrads, down_last, preferred_element_type=flt).astype(
         half
@@ -79,6 +74,26 @@
     )
     grad_firstw = jnp.einsum("trk,trc->rkc", inputs, grad_first, preferred_element_type=flt)
 
+    return encoded, grad_in, grad_firstw, grad_last
+
+
+def shards(tokens, up_first, up_mix, down_mix, down_last, cotangent):
+    mesh_sizes = {"core": 2, "y": 8, "zh": 4}
+    flt = jnp.float32
+    half = jnp.bfloat16
+    row_count = tokens.shape[0]
+    local_blocks = up_first.shape[0]
+    width_in = up_first.shape[1]
+    inputs = tokens.reshape(row_count, local_blocks, width_in)
+    outgrads = cotangent.reshape(row_count, local_blocks, width_in)
+    pieces = [
+        pipeline(inputs[rows], outgrads[rows], up_first, up_mix, down_mix, down_last)
+        for rows in (slice(i * row_count // CHUNKS, (i + 1) * row_count // CHUNKS) for i in range(CHUNKS))
+    ]
+    encoded = jnp.concatenate([piece[0] for piece in pieces], axis=0)
+    grad_in = jnp.concatenate([piece[1] for piece in pieces], axis=0)
+    grad_firstw = sum(piece[2] for piece in pieces[1:]) + pieces[0][2]
+    grad_last = sum(piece[3] for piece in pieces[1:]) + pieces[0][3]
     both = jnp.concatenate([grad_firstw.reshape(-1, grad_firstw.shape[-1]), grad_last.reshape(-1, grad_last.shape[-1])], axis=0)
     both = dp_sum(both, mesh_sizes)
     summed_first, summed_last = jnp.split(both, 2, axis=0)

time: 222 us -> 254 us (1.14)
  blocking collectives: 113 us -> 40.4 us
  starting transfers between devices: 11.3 us -> 49.4 us
  waiting for transfers between devices: 26.4 us -> 52.5 us
  local copies, waits for them, and re-layouts: 35.9 us -> 58.3 us
  matrix products: 28.6 us -> 42.1 us
    all_to_all x2 -> x0, blocking collectives: 74.6 us -> none  [the longest x1 47 us: to_blocks(): return lax.all_to_all(panel, BLK, split_axis=2, concat_axis=1, tiled=True)]
    all_to_all x0 -> x3, starting transfers between devices: none -> 29.9 us  [the longest x1 17.8 us: dp_sum(): total = lax.all_to_all(spread, DP_ORDER[-1], 0, 0, tiled=True).sum(axis=0)]
    all_to_all x0 -> x3, waiting for transfers between devices: none -> 26.5 us  [the longest x2 13.5 us: to_blocks(): return lax.all_to_all(panel, BLK, split_axis=2, concat_axis=1, tiled=True)]
    dot_general x9 -> x20, matrix products: 28.6 us -> 42.1 us  [the longest x2 12.8 us: pipeline(): jnp.einsum('tsc,cqs->tqc', hidden_tok, down_mix, preferred_element_type=flt)]
    convert_element_type x0 -> x4, local copies, waits for them, and re-layouts: none -> 9.85 us  [the longest x2 5.15 us: pipeline(): grad_pre_tok = (grad_hidden_tok.astype(flt) * slope).astype(half)]
    all_to_all x1 -> x2, starting transfers between devices: 7.83 us -> 16.1 us  [to_tokens(): return lax.all_to_all(panel, BLK, split_axis=1, concat_axis=2, tiled=True)]
    convert_element_type x0 -> x2, other arithmetic: none -> 4.89 us  [pipeline(): hidden_tok = hidden_f.astype(half)]
    dot_general x0 -> x4, local copies, waits for them, and re-layouts: none -> 4.87 us  [the longest x2 2.46 us: pipeline(): jnp.einsum('trc,csr->tsc', first_tok, up_mix, preferred_element_type=flt)]
  transfers between devices with their start and end apart: 2 -> 6, of which waited for: 2 -> 4; matrix products, arithmetic and copies ran while one was open for 9% -> 38% of each run, Pallas kernels for 0% -> 0%
where the time goes in v6:
time: 254 us; the launch traced here: 251 us
  local copies, waits for them, and re-layouts  58.3 us (23%)
  waiting for transfers between devices  52.5 us (21%)
  starting transfers between devices  49.4 us (19%)
  matrix products  42.1 us (17%)
  blocking collectives  40.4 us (16%)
  other arithmetic  7.54 us (3%)
    all_to_all x2, blocking collectives, dp_sum(): lax.all_to_all(total.reshape(count, -1, lanes), axis, 0, 0, tiled=True)  34.4 us
    unnamed x48, local copies, waits for them, and re-layouts  21.6 us
    all_to_all x1, starting transfers between devices, dp_sum(): total = lax.all_to_all(spread, DP_ORDER[-1], 0, 0, tiled=True).sum(axis=0)  17.8 us
    all_to_all x2, starting transfers between devices, to_tokens(): return lax.all_to_all(panel, BLK, split_axis=1, concat_axis=2, tiled=True)  16.1 us
    all_to_all x1, waiting for transfers between devices, dp_sum(): total = lax.all_to_all(spread, axis, 0, 0, tiled=True).reshape(-1, lanes)  13.5 us
    all_to_all x2, waiting for transfers between devices, to_blocks(): return lax.all_to_all(panel, BLK, split_axis=2, concat_axis=1, tiled=True)  13.5 us
    all_to_all x1, waiting for transfers between devices, dp_sum(): total = lax.all_to_all(spread, DP_ORDER[-1], 0, 0, tiled=True).sum(axis=0)  13 us
    dot_general x2, matrix products, pipeline(): jnp.einsum('tsc,cqs->tqc', hidden_tok, down_mix, preferred_element_type=flt)  12.8 us
  transfers between devices with their start and end apart: 6, of which 4 were waited for; matrix products, arithmetic and copies ran while one was open for 38% of the time, Pallas kernels for 0%

profile of v6, /device:TPU:7, one launch (start us, length us, event | category | flops | bytes accessed | tf_op | source)
XLA Modules:
  0.0 251.5 jit_solution(13294862877099882843)
XLA Ops:
  0.7 1.1 fusion.49
  3.2 1.5 copy.168
  4.6 7.8 %all-to-all-start.2 = ((bf16[2,144,8,256]{3,2,0,1:T(8,128)(2,1)}), bf16[2,144,8,256]{3,2,0,1:T(8,128)(2,1)S(1)}, u32[]{:S(2)}, u32[]{:S(2)}) async-start(bf16[2,144,8,256]{3,2,0,1:T(8,128)(2,1)} %copy.168), calls=%async_computation.2 | async-start | bytes 2359296 | tf_op jit(solution)/shard_map/all_to_all | solution.py:25
  13.7 1.4 copy.148
  15.1 12.4 %all-to-all-done.2 = bf16[2,144,8,256]{3,2,0,1:T(8,128)(2,1)S(1)} async-done(((bf16[2,144,8,256]{3,2,0,1:T(8,128)(2,1)}), bf16[2,144,8,256]{3,2,0,1:T(8,128)(2,1)S(1)}, u32[]{:S(2)}, u32[]{:S(2)}) %all-to-all-start.2) | async-done | bytes 1179680 | tf_op jit(solution)/shard_map/all_to_all | solution.py:25
  27.5 8.2 %all-to-all-start = ((bf16[2,144,8,256]{3,2,0,1:T(8,128)(2,1)}), bf16[2,144,8,256]{3,2,0,1:T(8,128)(2,1)S(1)}, u32[]{:S(2)}, u32[]{:S(2)}) async-start(bf16[2,144,8,256]{3,2,0,1:T(8,128)(2,1)} %copy.148), calls=%async_computation | async-start | bytes 2359296 | tf_op jit(solution)/shard_map/all_to_all | solution.py:25
  35.7 8.5 %copy.152 = bf16[256,96,96]{2,1,0:T(8,128)(2,1)} copy(bf16[256,96,96]{0,2,1:T(8,128)(2,1)} %param.8) | data formatting | bytes 9437184 | tf_op args[2]
  44.2 8.5 %copy.155 = bf16[256,96,96]{2,1,0:T(8,128)(2,1)} copy(bf16[256,96,96]{0,2,1:T(8,128)(2,1)} %param.9) | data formatting | bytes 9437184 | tf_op args[3]
  52.9 1.0 copy_bitcast_fusion.2
  53.8 1.0 copy.171
  54.8 6.1 %fusion.53 = bf16[256,12,96]{2,1,0:T(8,128)(2,1)S(1)} fusion(bf16[12,96,256]{1,0,2:T(8,128)(2,1)S(1)} %copy.171, bf16[256,96,96]{2,1,0:T(8,128)(2,1)} %copy.152), kind=kOutput, calls=%fused_computation.86 | convolution fusion | flops 56623104 | bytes 5898240 | tf_op jit(solution)/shard_map/trc,csr->tsc/dot_general | solution.py:56
  60.9 1.6 copy.173
  62.5 1.8 copy.177
  64.4 4.5 %fusion.54 = bf16[256,12,96]{2,1,0:T(8,128)(2,1)S(1)} fusion(bf16[12,96,256]{1,0,2:T(8,128)(2,1)S(1)} %copy.177, bf16[256,96,96]{2,1,0:T(8,128)(2,1)} %copy.155), kind=kOutput, calls=%fused_computation.87 | convolution fusion | flops 56623104 | bytes 5898240 | tf_op jit(solution)/shard_map/tqc,cqs->tsc/dot_general | solution.py:62
  68.9 1.5 copy.179
  70.4 3.0 %fusion.24 = (bf16[12,96,256]{2,1,0:T(8,128)(2,1)}, bf16[12,96,256]{2,1,0:T(8,128)(2,1)}) fusion(bf16[256,12,96]{0,2,1:T(8,128)(2,1)S(1)} %copy-done.3, bf16[256,12,96]{0,2,1:T(8,128)(2,1)} %copy.179), kind=kLoop, calls=%fused_computation.47 | loop fusion | flops 6782976 | bytes 2359296 | tf_op jit(solution)/shard_map/convert_element_type | solution.py:58
  73.4 2.7 %copy.174 = bf16[12,96,256]{1,0,2:T(8,128)(2,1)} copy(bf16[12,96,256]{2,1,0:T(8,128)(2,1)} %get-tuple-element.36) | data formatting | bytes 1179648 | tf_op jit(solution)/shard_map/convert_element_type | solution.py:58
  76.2 2.6 %copy.180 = bf16[12,96,256]{1,0,2:T(8,128)(2,1)} copy(bf16[12,96,256]{2,1,0:T(8,128)(2,1)} %get-tuple-element.37) | data formatting | bytes 1179648 | tf_op jit(solution)/shard_map/convert_element_type | solution.py:65
  78.7 6.6 %fusion.2 = bf16[1,12,96,256]{2,1,3,0:T(8,128)(2,1)S(1)} fusion(bf16[12,96,256]{1,0,2:T(8,128)(2,1)} %copy.174, bf16[256,96,96]{2,1,0:T(8,128)(2,1)} %copy.155), kind=kOutput, calls=%fused_computation.12 | convolution fusion | flops 56918016 | bytes 5898240 | tf_op jit(solution)/shard_map/tsc,cqs->tqc/dot_general | solution.py:59
  85.4 1.7 fusion.3
  87.7 3.2 %copy.182 = bf16[2,12,96,256]{3,0,1,2:T(2,128)(2,1)} copy(bf16[2,12,96,256]{2,1,3,0:T(8,128)(2,1)S(1)} %pad_maximum_fusion.1) | data formatting | bytes 2359296 | tf_op jit(solution)/shard_map/stack | solution.py:69
  90.9 6.1 %all-to-all-start.3 = ((bf16[2,12,96,256]{3,0,1,2:T(2,128)(2,1)}), bf16[2,12,96,256]{3,0,1,2:T(2,128)(2,1)}, u32[]{:S(2)}, u32[]{:S(2)}) async-start(bf16[2,12,96,256]{3,0,1,2:T(2,128)(2,1)} %copy.182), calls=%async_computation.3 | async-start | bytes 2359296 | tf_op jit(solution)/shard_map/all_to_all | solution.py:29
  97.2 1.0 copy.151
  98.3 6.1 %fusion.51 = bf16[256,12,96]{2,1,0:T(8,128)(2,1)S(1)} fusion(bf16[12,96,256]{1,0,2:T(8,128)(2,1)S(1)} %copy.151, bf16[256,96,96]{2,1,0:T(8,128)(2,1)} %copy.152), kind=kOutput, calls=%fused_computation.84 | convolution fusion | flops 56623104 | bytes 5898240 | tf_op jit(solution)/shard_map/trc,csr->tsc/dot_general | solution.py:56
  105.3 1.0 copy.157
  106.3 4.5 %fusion.52 = bf16[256,12,96]{2,1,0:T(8,128)(2,1)S(1)} fusion(bf16[12,96,256]{1,0,2:T(8,128)(2,1)S(1)} %copy.157, bf16[256,96,96]{2,1,0:T(8,128)(2,1)} %copy.155), kind=kOutput, calls=%fused_computation.85 | convolution fusion | flops 56623104 | bytes 5898240 | tf_op jit(solution)/shard_map/tqc,cqs->tsc/dot_general | solution.py:62
  111.7 1.9 fusion.28
  113.6 2.0 copy.154
  115.6 2.6 %copy.160 = bf16[12,96,256]{1,0,2:T(8,128)(2,1)} copy(bf16[12,96,256]{2,1,0:T(8,128)(2,1)} %get-tuple-element.35) | data formatting | bytes 1179648 | tf_op jit(solution)/shard_map/convert_element_type | solution.py:65
  118.1 6.3 %fusion = bf16[1,12,96,256]{2,1,3,0:T(8,128)(2,1)S(1)} fusion(bf16[12,96,256]{1,0,2:T(8,128)(2,1)S(1)} %copy.154, bf16[256,96,96]{2,1,0:T(8,128)(2,1)} %copy.155), kind=kOutput, calls=%fused_computation.10 | convolution fusion | flops 56918016 | bytes 5898240 | tf_op jit(solution)/shard_map/tsc,cqs->tqc/dot_general | solution.py:59
  124.5 1.7 fusion.1
  126.8 3.2 %copy.162 = bf16[2,12,96,256]{3,0,1,2:T(2,128)(2,1)} copy(bf16[2,12,96,256]{2,1,3,0:T(8,128)(2,1)S(1)} %pad_maximum_fusion) | data formatting | bytes 2359296 | tf_op jit(solution)/shard_map/stack | solution.py:69
  130.0 6.1 %all-to-all-start.1 = ((bf16[2,12,96,256]{3,0,1,2:T(2,128)(2,1)}), bf16[2,12,96,256]{3,0,1,2:T(2,128)(2,1)S(1)}, u32[]{:S(2)}, u32[]{:S(2)}) async-start(bf16[2,12,96,256]{3,0,1,2:T(2,128)(2,1)} %copy.162), calls=%async_computation.1 | async-start | bytes 2359296 | tf_op jit(solution)/shard_map/all_to_all | solution.py:29
  136.1 1.5 copy.218
  137.7 0.9 copy-done.7
  138.6 1.0 fusion.34
  139.7 13.5 %all-to-all-done.1 = bf16[2,12,96,256]{3,0,1,2:T(2,128)(2,1)S(1)} async-done(((bf16[2,12,96,256]{3,0,1,2:T(2,128)(2,1)}), bf16[2,12,96,256]{3,0,1,2:T(2,128)(2,1)S(1)}, u32[]{:S(2)}, u32[]{:S(2)}) %all-to-all-start.1) | async-done | bytes 1179680 | tf_op jit(solution)/shard_map/all_to_all | solution.py:29
  156.2 9.0 %all_to_all.85 = f32[2,512,256]{2,1,0:T(8,128)S(1)} all-to-all(f32[2,512,256]{2,1,0:T(8,128)S(1)} %bitcast.165), channel_id=1, replica_groups=mesh['y'=8,'zh'=4,'core'=2,'zl'=3,'x'=4] {'core'}, dimensions={0} | all-to-all | bytes 2097152 | tf_op jit(solution)/shard_map/all_to_all | solution.py:36
  165.2 0.9 reduce_sum.27
  166.1 25.4 %all_to_all.86 = f32[8,64,256]{2,1,0:T(8,128)S(1)} all-to-all(f32[8,64,256]{2,1,0:T(8,128)} %bitcast.183), channel_id=1, replica_groups=mesh['y'=8,'zh'=4,'core'=2,'zl'=3,'x'=4] {'y'}, dimensions={0} | all-to-all | bytes 1048576 | tf_op jit(solution)/shard_map/all_to_all | solution.py:36
  192.3 17.8 %all-to-all-start.6 = ((f32[4,64,256]{2,1,0:T(8,128)}), f32[4,64,256]{2,1,0:T(8,128)S(1)}, u32[]{:S(2)}, u32[]{:S(2)}) async-start(f32[4,64,256]{2,1,0:T(8,128)} %broadcast_in_dim.8), calls=%async_computation.6 | async-start | bytes 524288 | tf_op jit(solution)/shard_map/all_to_all | solution.py:40
  210.4 13.0 %all-to-all-done.6 = f32[4,64,256]{2,1,0:T(8,128)S(1)} async-done(((f32[4,64,256]{2,1,0:T(8,128)}), f32[4,64,256]{2,1,0:T(8,128)S(1)}, u32[]{:S(2)}, u32[]{:S(2)}) %all-to-all-start.6) | async-done | bytes 262176 | tf_op jit(solution)/shard_map/all_to_all | solution.py:40
  224.3 3.5 %all-to-all-start.7 = ((f32[8,64,256]{2,1,0:T(8,128)}), f32[8,64,256]{2,1,0:T(8,128)S(1)}, u32[]{:S(2)}, u32[]{:S(2)}) async-start(f32[8,64,256]{2,1,0:T(8,128)} %broadcast_in_dim.9), calls=%async_computation.7 | async-start | bytes 1048576 | tf_op jit(solution)/shard_map/all_to_all | solution.py:44
  228.3 0.9 copy.195
  230.0 0.9 copy.194
  230.9 13.5 %all-to-all-done.7 = f32[8,64,256]{2,1,0:T(8,128)S(1)} async-done(((f32[8,64,256]{2,1,0:T(8,128)}), f32[8,64,256]{2,1,0:T(8,128)S(1)}, u32[]{:S(2)}, u32[]{:S(2)}) %all-to-all-start.7) | async-done | bytes 524320 | tf_op jit(solution)/shard_map/all_to_all | solution.py:44
  244.5 6.0 %all_to_all.87 = f32[2,512,256]{2,1,0:T(8,128)S(1)} all-to-all(f32[2,512,256]{2,1,0:T(8,128)S(1)} %broadcast_in_dim.22), channel_id=1, replica_groups=mesh['y'=8,'zh'=4,'core'=2,'zl'=3,'x'=4] {'core'}, dimensions={0} | all-to-all | bytes 2097152 | tf_op jit(solution)/shard_map/all_to_all | solution.py:44
  250.4 1.0 fusion.48
  (89 shorter events, 12.2 us)
Async XLA Ops:
  0.6 1.4 copy-start
  0.6 1.2 copy-start.17
  1.7 1.0 copy-start.15
  1.9 1.2 copy-start.6
  2.1 1.1 copy-start.4
  4.6 22.8 %all-to-all-start.2 = ((bf16[2,144,8,256]{3,2,0,1:T(8,128)(2,1)}), bf16[2,144,8,256]{3,2,0,1:T(8,128)(2,1)S(1)}, u32[]{:S(2)}, u32[]{:S(2)}) async-start(bf16[2,144,8,256]{3,2,0,1:T(8,128)(2,1)} %copy.168), calls=%async_computation.2 | async-start | bytes 2359296 | tf_op jit(solution)/shard_map/all_to_all | solution.py:25
  12.6 0.9 copy-start.10
  12.8 0.9 copy-start.12
  27.5 63.4 %all-to-all-start = ((bf16[2,144,8,256]{3,2,0,1:T(8,128)(2,1)}), bf16[2,144,8,256]{3,2,0,1:T(8,128)(2,1)S(1)}, u32[]{:S(2)}, u32[]{:S(2)}) async-start(bf16[2,144,8,256]{3,2,0,1:T(8,128)(2,1)} %copy.148), calls=%async_computation | async-start | bytes 2359296 | tf_op jit(solution)/shard_map/all_to_all | solution.py:25
  68.9 1.6 copy-start.3
  73.4 11.9 %slice-start = ((s8[6291456]{0:T(1024)(128)(4,1)}), s8[2097152]{0:T(1024)(128)(4,1)S(1)}, s32[]{:S(2)}) async-start(s8[6291456]{0:T(1024)(128)(4,1)} %bitcast.157), calls=%async_computation.9 | async-start | bytes 4194304
  78.7 6.6 %slice-start.1 = ((s8[6291456]{0:T(1024)(128)(4,1)}), s8[4194304]{0:T(1024)(128)(4,1)S(1)}, s32[]{:S(2)}) async-start(s8[6291456]{0:T(1024)(128)(4,1)} %bitcast.157), calls=%async_computation.10 | async-start | bytes 8388608
  78.7 6.6 %copy-start.2 = (bf16[12,96,256]{1,0,2:T(8,128)(2,1)S(1)}, bf16[12,96,256]{1,0,2:T(8,128)(2,1)}, u32[]{:S(2)}) copy-start(bf16[12,96,256]{1,0,2:T(8,128)(2,1)} %copy.180) | copy-start | bytes 1769476
  90.9 39.1 %all-to-all-start.3 = ((bf16[2,12,96,256]{3,0,1,2:T(2,128)(2,1)}), bf16[2,12,96,256]{3,0,1,2:T(2,128)(2,1)}, u32[]{:S(2)}, u32[]{:S(2)}) async-start(bf16[2,12,96,256]{3,0,1,2:T(2,128)(2,1)} %copy.182), calls=%async_computation.3 | async-start | bytes 2359296 | tf_op jit(solution)/shard_map/all_to_all | solution.py:29
  113.6 10.8 %slice-start.2 = ((s8[6291456]{0:T(1024)(128)(4,1)}), s8[2097152]{0:T(1024)(128)(4,1)S(1)}, s32[]{:S(2)}) async-start(s8[6291456]{0:T(1024)(128)(4,1)} %bitcast.159), calls=%async_computation.11 | async-start | bytes 4194304
  118.1 6.3 %slice-start.3 = ((s8[6291456]{0:T(1024)(128)(4,1)}), s8[4194304]{0:T(1024)(128)(4,1)S(1)}, s32[]{:S(2)}) async-start(s8[6291456]{0:T(1024)(128)(4,1)} %bitcast.159), calls=%async_computation.12 | async-start | bytes 8388608
  118.1 6.3 %copy-start.1 = (bf16[12,96,256]{1,0,2:T(8,128)(2,1)S(1)}, bf16[12,96,256]{1,0,2:T(8,128)(2,1)}, u32[]{:S(2)}) copy-start(bf16[12,96,256]{1,0,2:T(8,128)(2,1)} %copy.160) | copy-start | bytes 1769476
  130.0 23.2 %all-to-all-start.1 = ((bf16[2,12,96,256]{3,0,1,2:T(2,128)(2,1)}), bf16[2,12,96,256]{3,0,1,2:T(2,128)(2,1)S(1)}, u32[]{:S(2)}, u32[]{:S(2)}) async-start(bf16[2,12,96,256]{3,0,1,2:T(2,128)(2,1)} %copy.162), calls=%async_computation.1 | async-start | bytes 2359296 | tf_op jit(solution)/shard_map/all_to_all | solution.py:29
  137.7 1.0 copy-start.7
  153.5 1.0 copy-start.5
  153.6 1.2 copy-start.8
  154.5 0.9 copy-start.11
  154.5 1.1 copy-start.14
  154.8 1.1 copy-start.13
  166.1 44.0 %copy-start.9 = (bf16[1,12,12,8,256]{4,3,2,1,0:T(8,128)(2,1)S(1)}, bf16[1,12,12,8,256]{4,3,2,1,0:T(8,128)(2,1)}, u32[]{:S(2)}) copy-start(bf16[1,12,12,8,256]{4,3,2,1,0:T(8,128)(2,1)} %copy-done.8) | copy-start | bytes 1769476
  192.3 31.2 %all-to-all-start.6 = ((f32[4,64,256]{2,1,0:T(8,128)}), f32[4,64,256]{2,1,0:T(8,128)S(1)}, u32[]{:S(2)}, u32[]{:S(2)}) async-start(f32[4,64,256]{2,1,0:T(8,128)} %broadcast_in_dim.8), calls=%async_computation.6 | async-start | bytes 524288 | tf_op jit(solution)/shard_map/all_to_all | solution.py:40
  224.3 20.1 %all-to-all-start.7 = ((f32[8,64,256]{2,1,0:T(8,128)}), f32[8,64,256]{2,1,0:T(8,128)S(1)}, u32[]{:S(2)}, u32[]{:S(2)}) async-start(f32[8,64,256]{2,1,0:T(8,128)} %broadcast_in_dim.9), calls=%async_computation.7 | async-start | bytes 1048576 | tf_op jit(solution)/shard_map/all_to_all | solution.py:44
  227.8 1.4 copy-start.16

commit v7 on v4

--- a/solution.py
+++ b/solution.py
@@ -30,15 +30,15 @@
 
 def dp_sum(total, sizes):
     lanes = total.shape[-1]
-    for axis in DP_ORDER:
-        count = sizes[axis]
-        pieces = lax.all_to_all(total.reshape(count, -1, lanes), axis, 0, 0, tiled=True)
-        total = pieces.sum(axis=0)
-    for axis in reversed(DP_ORDER):
-        count = sizes[axis]
-        spread = jnp.broadcast_to(total[None], (count,) + total.shape)
-        total = lax.all_to_all(spread, axis, 0, 0, tiled=True).reshape(-1, lanes)
-    return total
+    near = ("y", "core")
+    count = sizes["y"] * sizes["core"]
+    pieces = lax.all_to_all(total.reshape(count, -1, lanes), near, 0, 0, tiled=True)
+    total = pieces.sum(axis=0)
+    far = sizes["zh"]
+    spread = jnp.broadcast_to(total[None], (far,) + total.shape)
+    total = lax.all_to_all(spread, "zh", 0, 0, tiled=True).sum(axis=0)
+    spread = jnp.broadcast_to(total[None], (count,) + total.shape)
+    return lax.all_to_all(spread, near, 0, 0, tiled=True).reshape(-1, lanes)
 
 
 def shards(tokens, up_first, up_mix, down_mix, down_last, cotangent):

time: 232 us -> 239 us (1.030)
  waiting for transfers between devices: 23.1 us -> 40.3 us
  blocking collectives: 124 us -> 113 us
    all_to_all x1, waiting for transfers between devices: 8.11 us -> 25.4 us  [dp_sum(): return lax.all_to_all(spread, near, 0, 0, tiled=True).reshape(-1, lanes)]
    all_to_all x5 -> x2, blocking collectives: 77.3 us -> 66.4 us  [the longest x1 37.6 us: dp_sum(): lax.all_to_all(total.reshape(count, -1, lanes), near, 0, 0, tiled=True)]
    unnamed x18 -> x20, local copies, waits for them, and re-layouts: 21.5 us -> 21.6 us
  transfers between devices with their start and end apart: 2 -> 2, of which waited for: 2 -> 2; matrix products, arithmetic and copies ran while one was open for 9% -> 8% of each run, Pallas kernels for 0% -> 0%
where the time goes in v7:
time: 239 us; the launch traced here: 236 us
  blocking collectives  113 us (47%)
  waiting for transfers between devices  40.3 us (17%)
  local copies, waits for them, and re-layouts  37.5 us (16%)
  matrix products  27.6 us (12%)
  starting transfers between devices  12.3 us (5%)
  other arithmetic  4.19 us (2%)
    all_to_all x1, blocking collectives, to_blocks(): return lax.all_to_all(panel, BLK, split_axis=2, concat_axis=1, tiled=True)  47 us
    all_to_all x1, blocking collectives, dp_sum(): lax.all_to_all(total.reshape(count, -1, lanes), near, 0, 0, tiled=True)  37.6 us
    all_to_all x1, blocking collectives, dp_sum(): total = lax.all_to_all(spread, 'zh', 0, 0, tiled=True).sum(axis=0)  28.8 us
    all_to_all x1, waiting for transfers between devices, dp_sum(): return lax.all_to_all(spread, near, 0, 0, tiled=True).reshape(-1, lanes)  25.4 us
    unnamed x20, local copies, waits for them, and re-layouts  21.6 us
    all_to_all x1, waiting for transfers between devices, to_tokens(): return lax.all_to_all(panel, BLK, split_axis=1, concat_axis=2, tiled=True)  14.9 us
    dot_general x1, matrix products, shards(): jnp.einsum('tsc,csr->trc', grad_pre_tok, up_mix, preferred_element_type=flt)  10.1 us
    all_to_all x1, starting transfers between devices, to_tokens(): return lax.all_to_all(panel, BLK, split_axis=1, concat_axis=2, tiled=True)  7.83 us
  transfers between devices with their start and end apart: 2, of which 2 were waited for; matrix products, arithmetic and copies ran while one was open for 8% of the time, Pallas kernels for 0%

profile of v7, /device:TPU:7, one launch (start us, length us, event | category | flops | bytes accessed | tf_op | source)
XLA Modules:
  0.0 236.0 jit_solution(15270531195307663865)
XLA Ops:
  0.6 0.0 copy-start
  0.6 1.2 copy.67
  1.9 0.0 copy-start.3
  1.9 1.3 copy.68
  3.2 0.0 copy-start.1
  3.2 1.6 fusion.29
  4.8 0.0 copy-done
  4.8 0.5 fusion.28
  5.4 0.2 pad_maximum_fusion.1
  5.6 0.0 copy-done.3
  5.6 2.7 %copy.69 = bf16[2,288,8,256]{3,2,0,1:T(8,128)(2,1)} copy(bf16[2,288,8,256]{3,1,2,0:T(8,128)(2,1)S(1)} %pad_maximum_fusion.1) | data formatting | bytes 4718592 | tf_op jit(solution)/shard_map/stack | solution.py:57
  8.4 7.8 %all-to-all-start = ((bf16[2,288,8,256]{3,2,0,1:T(8,128)(2,1)}), bf16[2,288,8,256]{3,2,0,1:T(8,128)(2,1)S(1)}, u32[]{:S(2)}, u32[]{:S(2)}) async-start(bf16[2,288,8,256]{3,2,0,1:T(8,128)(2,1)} %copy.69), calls=%async_computation | async-start | bytes 4718592 | tf_op jit(solution)/shard_map/all_to_all | solution.py:24
  16.2 8.5 %copy.73 = bf16[256,96,96]{2,1,0:T(8,128)(2,1)} copy(bf16[256,96,96]{0,2,1:T(8,128)(2,1)} %param.8) | data formatting | bytes 9437184 | tf_op args[2]
  24.7 8.4 %copy.74 = bf16[256,96,96]{2,1,0:T(8,128)(2,1)} copy(bf16[256,96,96]{0,2,1:T(8,128)(2,1)} %param.9) | data formatting | bytes 9437184 | tf_op args[3]
  33.1 14.9 %all-to-all-done = bf16[2,288,8,256]{3,2,0,1:T(8,128)(2,1)S(1)} async-done(((bf16[2,288,8,256]{3,2,0,1:T(8,128)(2,1)}), bf16[2,288,8,256]{3,2,0,1:T(8,128)(2,1)S(1)}, u32[]{:S(2)}, u32[]{:S(2)}) %all-to-all-start) | async-done | bytes 2359328 | tf_op jit(solution)/shard_map/all_to_all | solution.py:24
  48.0 0.2 copy.70
  48.2 0.2 fusion.40
  48.4 0.3 copy_bitcast_fusion.1
  48.7 1.9 copy.76
  50.6 1.3 copy.72
  51.8 6.1 %convolution_convert_fusion.3 = bf16[256,24,96]{2,1,0:T(8,128)(2,1)S(1)} fusion(bf16[24,96,256]{1,0,2:T(8,128)(2,1)S(1)} %copy.72, bf16[256,96,96]{2,1,0:T(8,128)(2,1)} %copy.73), kind=kOutput, calls=%fused_computation.20 | convolution fusion | flops 113836032 | bytes 7077888 | tf_op jit(solution)/shard_map/trc,csr->tsc/dot_general | solution.py:58
  58.0 7.4 %fusion.22 = bf16[1,24,96,256]{2,1,3,0:T(8,128)(2,1)} fusion(bf16[256,96,96]{2,1,0:T(8,128)(2,1)} %copy.74, bf16[256,24,96]{2,1,0:T(8,128)(2,1)S(1)} %convolution_convert_fusion.3), kind=kOutput, calls=%fused_computation.32 | convolution fusion | flops 119734272 | bytes 7077888 | tf_op jit(solution)/shard_map/tsc,cqs->tqc/dot_general | solution.py:61
  65.4 0.0 copy-done.5
  65.4 10.1 %fusion.25 = bf16[1,24,96,256]{2,1,3,0:T(8,128)(2,1)} fusion(bf16[256,96,96]{2,1,0:T(8,128)(2,1)} %copy.73, bf16[256,24,96]{2,1,0:T(8,128)(2,1)S(1)} %convolution_convert_fusion.3, bf16[24,96,256]{1,0,2:T(8,128)(2,1)S(1)} %copy-done.5, bf16[256,96,96]{2,1,0:T(8,128)(2,1)} %copy.74), kind=kOutput, calls=%fused_computation.33 | convolution fusion | flops 240058368 | bytes 12976128 | tf_op jit(solution)/shard_map/tsc,csr->trc/dot_general | solution.py:68
  75.5 2.6 %pad_maximum_fusion = bf16[2,24,96,256]{2,1,3,0:T(8,128)(2,1)S(1)} fusion(bf16[1,24,96,256]{2,1,3,0:T(8,128)(2,1)} %fusion.25, bf16[1,24,96,256]{2,1,3,0:T(8,128)(2,1)} %fusion.22), kind=kLoop, calls=%fused_computation.9 | loop fusion | flops 1179648 | bytes 4718592 | tf_op jit(solution)/shard_map/stack | solution.py:71
  78.1 3.6 %copy.79 = bf16[2,24,96,256]{3,1,0,2:T(8,128)(2,1)} copy(bf16[2,24,96,256]{2,1,3,0:T(8,128)(2,1)S(1)} %pad_maximum_fusion) | data formatting | bytes 4718592 | tf_op jit(solution)/shard_map/stack | solution.py:71
  81.8 47.0 %all_to_all.45 = bf16[2,24,96,256]{3,1,0,2:T(8,128)(2,1)S(1)} all-to-all(bf16[2,24,96,256]{3,1,0,2:T(8,128)(2,1)} %copy.79), channel_id=1, replica_groups=mesh['y'=8,'zh'=4,'core'=2,'zl'=3,'x'=4] {'zl','x'}, dimensions={2} | all-to-all | bytes 4718592 | tf_op jit(solution)/shard_map/all_to_all | solution.py:28
  128.7 0.9 copy.88
  129.6 0.2 fusion.39
  129.7 0.0 copy-start.4
  129.8 0.7 copy.82
  130.4 0.0 copy-start.2
  130.4 0.3 copy-done.4
  130.7 0.4 fusion.42
  131.1 0.7 copy.81
  131.8 0.4 fusion.43
  132.2 0.1 pad_maximum_fusion.2
  132.3 37.6 %all_to_all.46 = f32[16,64,256]{2,1,0:T(8,128)} all-to-all(f32[16,64,256]{2,1,0:T(8,128)S(1)} %bitcast.98), channel_id=1, replica_groups=mesh['y'=8,'zh'=4,'core'=2,'zl'=3,'x'=4] {'y','core'}, dimensions={0} | all-to-all | bytes 2097152 | tf_op jit(solution)/shard_map/all_to_all | solution.py:35
  169.9 1.3 reduce_sum.18
  171.2 28.8 %all_to_all.47 = f32[4,64,256]{2,1,0:T(8,128)S(1)} all-to-all(f32[4,64,256]{2,1,0:T(8,128)S(1)} %broadcast_in_dim.4), channel_id=1, replica_groups=mesh['y'=8,'zh'=4,'core'=2,'zl'=3,'x'=4] {'zh'}, dimensions={0} | all-to-all | bytes 524288 | tf_op jit(solution)/shard_map/all_to_all | solution.py:39
  200.0 1.1 broadcast_in_dim.5
  201.1 4.5 %all-to-all-start.4 = ((f32[16,64,256]{2,1,0:T(8,128)}), f32[16,64,256]{2,1,0:T(8,128)}, u32[]{:S(2)}, u32[]{:S(2)}) async-start(f32[16,64,256]{2,1,0:T(8,128)} %broadcast_in_dim.5), calls=%async_computation.4 | async-start | bytes 2097152 | tf_op jit(solution)/shard_map/all_to_all | solution.py:41
  205.6 0.5 convolution_convert_fusion.6
  206.1 0.9 copy.84
  207.0 0.5 convolution_convert_fusion.7
  207.5 0.9 copy.83
  208.3 25.4 %all-to-all-done.4 = f32[16,64,256]{2,1,0:T(8,128)} async-done(((f32[16,64,256]{2,1,0:T(8,128)}), f32[16,64,256]{2,1,0:T(8,128)}, u32[]{:S(2)}, u32[]{:S(2)}) %all-to-all-start.4) | async-done | bytes 1048608 | tf_op jit(solution)/shard_map/all_to_all | solution.py:41
  233.7 2.3 fusion.41
  (7 shorter events, 0.0 us)
Async XLA Ops:
  0.6 4.2 %copy-start = (bf16[8,64,256]{2,1,0:T(8,128)(2,1)S(1)}, bf16[8,64,256]{2,1,0:T(8,128)(2,1)}, u32[]{:S(2)}) copy-start(bf16[8,64,256]{2,1,0:T(8,128)(2,1)} %param.7) | copy-start | bytes 786436
  1.9 3.7 %copy-start.3 = (bf16[288,512]{0,1:T(8,128)(2,1)}, bf16[288,512]{0,1:T(8,128)(2,1)S(1)}, u32[]{:S(2)}) copy-start(bf16[288,512]{0,1:T(8,128)(2,1)S(1)} %copy.67) | copy-start | bytes 884740
  3.2 2.4 %copy-start.1 = (bf16[288,512]{0,1:T(8,128)(2,1)}, bf16[288,512]{0,1:T(8,128)(2,1)S(1)}, u32[]{:S(2)}) copy-start(bf16[288,512]{0,1:T(8,128)(2,1)S(1)} %copy.68) | copy-start | bytes 884740
  8.4 39.7 %all-to-all-start = ((bf16[2,288,8,256]{3,2,0,1:T(8,128)(2,1)}), bf16[2,288,8,256]{3,2,0,1:T(8,128)(2,1)S(1)}, u32[]{:S(2)}, u32[]{:S(2)}) async-start(bf16[2,288,8,256]{3,2,0,1:T(8,128)(2,1)} %copy.69), calls=%async_computation | async-start | bytes 4718592 | tf_op jit(solution)/shard_map/all_to_all | solution.py:24
  58.0 7.5 %copy-start.5 = (bf16[24,96,256]{1,0,2:T(8,128)(2,1)S(1)}, bf16[24,96,256]{1,0,2:T(8,128)(2,1)}, u32[]{:S(2)}) copy-start(bf16[24,96,256]{1,0,2:T(8,128)(2,1)} %copy.76) | copy-start | bytes 3538948
  129.7 1.0 copy-start.4
  130.4 1.4 copy-start.2
  201.1 5.8 %copy-start.6 = (bf16[8,64,256]{2,1,0:T(8,128)(2,1)S(1)}, bf16[8,64,256]{2,1,0:T(8,128)(2,1)}, u32[]{:S(2)}) copy-start(bf16[8,64,256]{2,1,0:T(8,128)(2,1)} %param.10) | copy-start | bytes 786436
  201.1 32.6 %all-to-all-start.4 = ((f32[16,64,256]{2,1,0:T(8,128)}), f32[16,64,256]{2,1,0:T(8,128)}, u32[]{:S(2)}, u32[]{:S(2)}) async-start(f32[16,64,256]{2,1,0:T(8,128)} %broadcast_in_dim.5), calls=%async_computation.4 | async-start | bytes 2097152 | tf_op jit(solution)/shard_map/all_to_all | solution.py:41

commit v8 on v5

--- a/solution.py
+++ b/solution.py
@@ -5,6 +5,7 @@
 DP = ("y", "zh", "core")
 BLK = ("zl", "x")
 DP_ORDER = ("core", "y", "zh")
+ZL, XS = 3, 4
 
 gelu_coef = 0.7978845608028654
 cubic_coef = 0.044715
@@ -20,12 +21,22 @@
     return (result, slope)
 
 
-def to_tokens(panel):
-    return lax.all_to_all(panel, BLK, split_axis=1, concat_axis=2, tiled=True)
+def to_mixing(panel):
+    pair, rows, blocks, hidden = panel.shape
+    part = hidden // XS
+    panel = panel.reshape(pair, ZL, rows // ZL, blocks, XS, part).transpose(0, 1, 4, 2, 3, 5)
+    panel = panel.reshape(pair, ZL * XS, rows // ZL, blocks, part)
+    panel = lax.all_to_all(panel, BLK, split_axis=1, concat_axis=3, tiled=True)
+    return panel.reshape(pair, rows // ZL, blocks * ZL * XS, part).transpose(0, 3, 1, 2)
 
 
-def to_blocks(panel):
-    return lax.all_to_all(panel, BLK, split_axis=2, concat_axis=1, tiled=True)
+def from_mixing(panel):
+    pair, part, rows, width = panel.shape
+    blocks = width // (ZL * XS)
+    panel = panel.reshape(pair, part, rows, ZL * XS, blocks).transpose(0, 3, 1, 2, 4)
+    panel = lax.all_to_all(panel, BLK, split_axis=1, concat_axis=1, tiled=True)
+    panel = panel.reshape(pair, ZL, XS, part, rows, blocks).transpose(0, 1, 4, 5, 2, 3)
+    return panel.reshape(pair, ZL * rows, blocks, XS * part)
 
 
 def dp_sum(total, sizes):
@@ -57,21 +68,25 @@
     grad_mixed = jnp.einsum("tqk,qkc->tqc", outgrads, down_last, preferred_element_type=flt).astype(
         half
     )
-    first_tok, grad_mixed_tok = to_tokens(jnp.stack([first, grad_mixed]))
-    pre_tok = jnp.einsum("trc,csr->tsc", first_tok, up_mix, preferred_element_type=flt).astype(half)
-    hidden_f, slope = gelu_pair(pre_tok.astype(flt))
-    hidden_tok = hidden_f.astype(half)
-    mixed_tok = jnp.einsum("tsc,cqs->tqc", hidden_tok, down_mix, preferred_element_type=flt).astype(
+    part = up_mix.shape[0] // XS
+    column = lax.axis_index("x") * part
+    up_mix_l = lax.dynamic_slice_in_dim(up_mix, column, part, axis=0)
+    down_mix_l = lax.dynamic_slice_in_dim(down_mix, column, part, axis=0)
+    first_m, grad_mixed_m = to_mixing(jnp.stack([first, grad_mixed]))
+    pre_m = jnp.einsum("ctr,csr->cts", first_m, up_mix_l, preferred_element_type=flt).astype(half)
+    hidden_f, slope = gelu_pair(pre_m.astype(flt))
+    hidden_m = hidden_f.astype(half)
+    mixed_m = jnp.einsum("cts,cqs->ctq", hidden_m, down_mix_l, preferred_element_type=flt).astype(
         half
     )
-    grad_hidden_tok = jnp.einsum(
-        "tqc,cqs->tsc", grad_mixed_tok, down_mix, preferred_element_type=flt
+    grad_hidden_m = jnp.einsum(
+        "ctq,cqs->cts", grad_mixed_m, down_mix_l, preferred_element_type=flt
     ).astype(half)
-    grad_pre_tok = (grad_hidden_tok.astype(flt) * slope).astype(half)
-    grad_first_tok = jnp.einsum(
-        "tsc,csr->trc", grad_pre_tok, up_mix, preferred_element_type=flt
+    grad_pre_m = (grad_hidden_m.astype(flt) * slope).astype(half)
+    grad_first_m = jnp.einsum(
+        "cts,csr->ctr", grad_pre_m, up_mix_l, preferred_element_type=flt
     ).astype(half)
-    mixed, grad_first = to_blocks(jnp.stack([mixed_tok, grad_first_tok]))
+    mixed, grad_first = from_mixing(jnp.stack([mixed_m, grad_first_m]))
     encoded = jnp.einsum("tqc,qkc->tqk", mixed, down_last, preferred_element_type=flt).astype(half)
     grad_last = jnp.einsum("tqk,tqc->qkc", outgrads, mixed, preferred_element_type=flt)
     grad_in = jnp.einsum("trc,rkc->trk", grad_first, up_first, preferred_element_type=flt).astype(

time: 222 us -> 276 us (1.24)
  local copies, waits for them, and re-layouts: 35.9 us -> 68.1 us
  waiting for transfers between devices: 26.4 us -> 38.9 us
  blocking collectives: 113 us -> 125 us
  matrix products: 28.6 us -> 18.8 us
  other arithmetic: 5.32 us -> 10.9 us
    another operation x9 -> x7, local copies, waits for them, and re-layouts: 11.4 us -> 24.6 us  [the longest x5 16.4 us: shards(): mixed, grad_first = from_mixing(jnp.stack([mixed_m, grad_first_m]))]
    all_to_all x1, waiting for transfers between devices: 15 us -> 27.9 us  [to_mixing(): panel = lax.all_to_all(panel, BLK, split_axis=1, concat_axis=3, tiled=True)]
    reshape x0 -> x2, local copies, waits for them, and re-layouts: none -> 12.3 us  [the longest x1 7.48 us: to_mixing(): panel = panel.reshape(pair, ZL * XS, rows // ZL, blocks, part)]
    all_to_all x1, blocking collectives: 47 us -> 58.8 us  [from_mixing(): panel = lax.all_to_all(panel, BLK, split_axis=1, concat_axis=1, tiled=True)]
    dot_general x3, matrix products: 23.7 us -> 13.2 us  [the longest x1 6.24 us: shards(): jnp.einsum('cts,csr->ctr', grad_pre_m, up_mix_l, preferred_element_type=flt)]
    transpose x0 -> x2, other arithmetic: none -> 8.43 us  [the longest x1 7.72 us: to_mixing(): panel.reshape(pair, ZL, rows // ZL, blocks, XS, part)]
    unnamed x18, local copies, waits for them, and re-layouts: 21.5 us -> 13.7 us
    convert_element_type x0 -> x4, local copies, waits for them, and re-layouts: none -> 6.07 us  [the longest x1 1.86 us: shards(): grad_first_m = jnp.einsum('cts,csr->ctr', grad_pre_m, up_mix_l, preferred...]
  transfers between devices with their start and end apart: 2 -> 2, of which waited for: 2 -> 2; matrix products, arithmetic and copies ran while one was open for 9% -> 7% of each run, Pallas kernels for 0% -> 0%
where the time goes in v8:
time: 276 us; the launch traced here: 274 us
  blocking collectives  125 us (45%)
  local copies, waits for them, and re-layouts  68.1 us (25%)
  waiting for transfers between devices  38.9 us (14%)
  matrix products  18.8 us (7%)
  starting transfers between devices  11.3 us (4%)
  other arithmetic  10.9 us (4%)
    all_to_all x1, blocking collectives, from_mixing(): panel = lax.all_to_all(panel, BLK, split_axis=1, concat_axis=1, tiled=True)  58.8 us
    all_to_all x2, blocking collectives, dp_sum(): lax.all_to_all(total.reshape(count, -1, lanes), axis, 0, 0, tiled=True)  29.8 us
    all_to_all x1, blocking collectives, dp_sum(): total = lax.all_to_all(spread, DP_ORDER[-1], 0, 0, tiled=True).sum(axis=0)  28.6 us
    all_to_all x1, waiting for transfers between devices, to_mixing(): panel = lax.all_to_all(panel, BLK, split_axis=1, concat_axis=3, tiled=True)  27.9 us
    another operation x5, local copies, waits for them, and re-layouts, shards(): mixed, grad_first = from_mixing(jnp.stack([mixed_m, grad_first_m]))  16.4 us
    unnamed x18, local copies, waits for them, and re-layouts  13.7 us
    all_to_all x1, waiting for transfers between devices, dp_sum(): total = lax.all_to_all(spread, axis, 0, 0, tiled=True).reshape(-1, lanes)  11 us
    another operation x2, local copies, waits for them, and re-layouts, shards(): first_m, grad_mixed_m = to_mixing(jnp.stack([first, grad_mixed]))  8.16 us
  transfers between devices with their start and end apart: 2, of which 2 were waited for; matrix products, arithmetic and copies ran while one was open for 7% of the time, Pallas kernels for 0%

profile of v8, /device:TPU:7, one launch (start us, length us, event | category | flops | bytes accessed | tf_op | source)
XLA Modules:
  0.0 274.0 jit_solution(7640456092580810993)
XLA Ops:
  0.6 1.2 copy.60
  1.9 1.3 copy.62
  3.2 1.6 fusion.22
  4.8 1.7 copy.63
  6.5 3.6 %stack.19 = bf16[1,3,96,8,4,64]{5,4,3,2,1,0:T(4,128)(2,1)S(1)} reshape(bf16[288,8,256]{2,1,0:T(8,128)(2,1)} %copy.63) | data formatting | bytes 2359296 | tf_op jit(solution)/shard_map/stack | solution.py:75
  10.1 0.5 fusion.21
  10.7 1.7 copy.61
  12.3 4.6 %stack.18 = bf16[1,3,96,8,4,64]{5,4,3,2,1,0:T(4,128)(2,1)} reshape(bf16[288,8,256]{2,1,0:T(8,128)(2,1)} %copy.61) | data formatting | bytes 2359296 | tf_op jit(solution)/shard_map/stack | solution.py:75
  16.9 7.7 %maximum_bitcast_fusion = bf16[2,3,4,96,8,64]{5,2,4,3,1,0:T(4,128)(2,1)} fusion(bf16[1,3,96,8,4,64]{5,4,3,2,1,0:T(4,128)(2,1)S(1)} %stack.19, bf16[1,3,96,8,4,64]{5,4,3,2,1,0:T(4,128)(2,1)} %stack.18), kind=kLoop, calls=%fused_computation.7 | loop fusion | flops 1179648 | bytes 4718592 | tf_op jit(solution)/shard_map/transpose | solution.py:27
  24.6 7.5 %copy.82 = bf16[2,3,4,96,8,64]{3,5,4,0,2,1:T(8,128)(2,1)} copy(bf16[2,3,4,96,8,64]{5,2,4,3,1,0:T(4,128)(2,1)} %maximum_bitcast_fusion) | data formatting | bytes 4718592 | tf_op jit(solution)/shard_map/reshape | solution.py:28
  32.1 7.8 %all-to-all-start = ((bf16[2,12,96,8,64]{2,4,3,0,1:T(8,128)(2,1)}), bf16[2,12,96,8,64]{2,4,3,0,1:T(8,128)(2,1)S(1)}, u32[]{:S(2)}, u32[]{:S(2)}) async-start(bf16[2,12,96,8,64]{2,4,3,0,1:T(8,128)(2,1)} %bitcast.72), calls=%async_computation | async-start | bytes 6291456 | tf_op jit(solution)/shard_map/all_to_all | solution.py:29
  39.9 5.8 %constant_dynamic-slice_fusion = (bf16[64,96,96]{0,2,1:T(8,128)(2,1)}, bf16[64,96,96]{0,2,1:T(8,128)(2,1)}) fusion(bf16[256,96,96]{0,2,1:T(8,128)(2,1)} %param.9, s32[]{:T(128)S(6)} %select_n.4, bf16[256,96,96]{0,2,1:T(8,128)(2,1)} %param.8), kind=kLoop, calls=%fused_computation.41 | loop fusion | bytes 4718596 | tf_op jit(solution)/shard_map/dynamic_slice | solution.py:74
  45.7 4.7 %copy.88 = bf16[64,96,96]{2,1,0:T(8,128)(2,1)} copy(bf16[64,96,96]{0,2,1:T(8,128)(2,1)} %get-tuple-element.24) | data formatting | bytes 2359296
  50.4 4.7 %copy.87 = bf16[64,96,96]{2,1,0:T(8,128)(2,1)} copy(bf16[64,96,96]{0,2,1:T(8,128)(2,1)} %get-tuple-element.25) | data formatting | bytes 2359296
  55.1 27.9 %all-to-all-done = bf16[2,12,96,8,64]{2,4,3,0,1:T(8,128)(2,1)S(1)} async-done(((bf16[2,12,96,8,64]{2,4,3,0,1:T(8,128)(2,1)}), bf16[2,12,96,8,64]{2,4,3,0,1:T(8,128)(2,1)S(1)}, u32[]{:S(2)}, u32[]{:S(2)}) %all-to-all-start) | async-done | bytes 2359328 | tf_op jit(solution)/shard_map/all_to_all | solution.py:29
  83.0 2.6 copy.66
  85.6 4.8 %copy.67 = bf16[2,96,96,64]{2,1,3,0:T(8,128)(2,1)S(1)} copy(bf16[2,96,96,64]{1,3,2,0:T(8,128)(2,1)} %bitcast.71) | data formatting | bytes 4718592 | tf_op jit(solution)/shard_map/reshape | solution.py:30
  90.4 3.8 %convolution_convert_fusion.3 = bf16[64,96,96]{2,1,0:T(8,128)(2,1)} fusion(bf16[64,96,96]{2,1,0:T(8,128)(2,1)} %copy.87, bf16[2,64,96,96]{3,2,1,0:T(8,128)(2,1)S(1)} %bitcast.73), kind=kOutput, calls=%fused_computation.23 | convolution fusion | flops 113836032 | bytes 3932160 | tf_op jit(solution)/shard_map/ctr,csr->cts/dot_general | solution.py:76
  94.2 6.2 %convolution_convert_fusion = bf16[64,96,96]{2,1,0:T(8,128)(2,1)} fusion(bf16[64,96,96]{2,1,0:T(8,128)(2,1)} %copy.87, bf16[64,96,96]{2,1,0:T(8,128)(2,1)} %convolution_convert_fusion.3, bf16[64,96,96]{2,1,0:T(8,128)(2,1)} %copy.88, bf16[2,64,96,96]{3,2,1,0:T(8,128)(2,1)S(1)} %bitcast.74), kind=kOutput, calls=%fused_computation.20 | convolution fusion | flops 240058368 | bytes 6291456 | tf_op jit(solution)/shard_map/cts,csr->ctr/dot_general | solution.py:86
  100.4 3.1 %convolution_convert_fusion.2 = bf16[64,96,96]{2,1,0:T(8,128)(2,1)S(1)} fusion(bf16[64,96,96]{2,1,0:T(8,128)(2,1)} %copy.88, bf16[64,96,96]{2,1,0:T(8,128)(2,1)} %convolution_convert_fusion.3), kind=kOutput, calls=%fused_computation.22 | convolution fusion | flops 119734272 | bytes 3538944 | tf_op jit(solution)/shard_map/cts,cqs->ctq/dot_general | solution.py:79
  103.6 0.9 copy.70
  104.5 1.9 copy.71
  106.3 0.7 maximum_bitcast_fusion.1
  107.0 0.9 copy.72
  107.9 58.8 %all_to_all.45 = bf16[2,12,64,96,8]{3,4,2,0,1:T(8,128)(2,1)S(1)} all-to-all(bf16[2,12,64,96,8]{3,4,2,0,1:T(8,128)(2,1)S(1)} %copy.72), channel_id=1, replica_groups=mesh['y'=8,'zh'=4,'core'=2,'zl'=3,'x'=4] {'zl','x'}, dimensions={1} | all-to-all | bytes 4718592 | tf_op jit(solution)/shard_map/all_to_all | solution.py:37
  166.7 0.3 copy.73
  167.0 1.4 fusion.32
  168.4 4.5 %copy.84 = bf16[1,3,96,8,4,64]{5,4,2,1,3,0:T(4,128)(2,1)} copy(bf16[1,3,96,8,4,64]{2,3,5,4,1,0:T(8,128)(2,1)} %get-tuple-element.20) | data formatting | bytes 2359296 | tf_op jit(solution)/shard_map/unstack | solution.py:89
  172.9 3.8 %reshape.85 = bf16[288,8,256]{2,0,1:T(8,128)(2,1)S(1)} reshape(bf16[1,3,96,8,4,64]{5,4,2,1,3,0:T(4,128)(2,1)} %copy.84) | data formatting | bytes 2359296 | tf_op jit(solution)/shard_map/unstack | solution.py:89
  176.7 1.2 fusion.34
  177.9 2.9 %copy.83 = bf16[1,3,96,8,4,64]{5,4,2,1,3,0:T(4,128)(2,1)} copy(bf16[1,3,96,8,4,64]{2,3,5,4,1,0:T(8,128)(2,1)S(1)} %get-tuple-element.21) | data formatting | bytes 2359296 | tf_op jit(solution)/shard_map/unstack | solution.py:89
  180.8 3.8 %reshape.84 = bf16[288,8,256]{2,0,1:T(8,128)(2,1)S(1)} reshape(bf16[1,3,96,8,4,64]{5,4,2,1,3,0:T(4,128)(2,1)} %copy.83) | data formatting | bytes 2359296 | tf_op jit(solution)/shard_map/unstack | solution.py:89
  184.6 0.4 fusion.35
  185.0 0.1 pad_maximum_fusion
  185.1 6.9 %all_to_all.46 = f32[2,512,256]{2,1,0:T(8,128)} all-to-all(f32[2,512,256]{2,1,0:T(8,128)S(1)} %bitcast.77), channel_id=1, replica_groups=mesh['y'=8,'zh'=4,'core'=2,'zl'=3,'x'=4] {'core'}, dimensions={0} | all-to-all | bytes 2097152 | tf_op jit(solution)/shard_map/all_to_all | solution.py:46
  192.0 1.4 reduce_sum.27
  193.4 22.8 %all_to_all.47 = f32[8,64,256]{2,1,0:T(8,128)} all-to-all(f32[8,64,256]{2,1,0:T(8,128)S(1)} %bitcast.83), channel_id=1, replica_groups=mesh['y'=8,'zh'=4,'core'=2,'zl'=3,'x'=4] {'y'}, dimensions={0} | all-to-all | bytes 1048576 | tf_op jit(solution)/shard_map/all_to_all | solution.py:46
  216.2 1.1 reduce_sum.28
  217.3 28.6 %all_to_all.48 = f32[4,64,256]{2,1,0:T(8,128)S(1)} all-to-all(f32[4,64,256]{2,1,0:T(8,128)S(1)} %broadcast_in_dim.8), channel_id=1, replica_groups=mesh['y'=8,'zh'=4,'core'=2,'zl'=3,'x'=4] {'zh'}, dimensions={0} | all-to-all | bytes 524288 | tf_op jit(solution)/shard_map/all_to_all | solution.py:50
  246.0 0.8 broadcast_in_dim.9
  246.8 3.5 %all-to-all-start.5 = ((f32[8,64,256]{2,1,0:T(8,128)}), f32[8,64,256]{2,1,0:T(8,128)S(1)}, u32[]{:S(2)}, u32[]{:S(2)}) async-start(f32[8,64,256]{2,1,0:T(8,128)} %broadcast_in_dim.9), calls=%async_computation.5 | async-start | bytes 1048576 | tf_op jit(solution)/shard_map/all_to_all | solution.py:54
  250.3 0.5 convolution_convert_fusion.6
  250.8 0.9 copy.81
  251.7 1.4 convolution_convert_fusion.7
  253.1 0.9 copy.80
  254.0 11.0 %all-to-all-done.5 = f32[8,64,256]{2,1,0:T(8,128)S(1)} async-done(((f32[8,64,256]{2,1,0:T(8,128)}), f32[8,64,256]{2,1,0:T(8,128)S(1)}, u32[]{:S(2)}, u32[]{:S(2)}) %all-to-all-start.5) | async-done | bytes 524320 | tf_op jit(solution)/shard_map/all_to_all | solution.py:54
  265.2 7.8 %all_to_all.49 = f32[2,512,256]{2,1,0:T(8,128)S(1)} all-to-all(f32[2,512,256]{2,1,0:T(8,128)S(1)} %broadcast_in_dim.22), channel_id=1, replica_groups=mesh['y'=8,'zh'=4,'core'=2,'zl'=3,'x'=4] {'core'}, dimensions={0} | all-to-all | bytes 2097152 | tf_op jit(solution)/shard_map/all_to_all | solution.py:54
  273.0 1.0 fusion.33
  (15 shorter events, 0.1 us)
Async XLA Ops:
  0.6 9.5 %copy-start = (bf16[8,64,256]{2,1,0:T(8,128)(2,1)S(1)}, bf16[8,64,256]{2,1,0:T(8,128)(2,1)}, u32[]{:S(2)}) copy-start(bf16[8,64,256]{2,1,0:T(8,128)(2,1)} %param.7) | copy-start | bytes 786436
  1.9 8.3 %copy-start.3 = (bf16[288,512]{0,1:T(8,128)(2,1)}, bf16[288,512]{0,1:T(8,128)(2,1)S(1)}, u32[]{:S(2)}) copy-start(bf16[288,512]{0,1:T(8,128)(2,1)S(1)} %copy.60) | copy-start | bytes 884740
  3.2 1.6 copy-start.1
  32.1 50.9 %all-to-all-start = ((bf16[2,12,96,8,64]{2,4,3,0,1:T(8,128)(2,1)}), bf16[2,12,96,8,64]{2,4,3,0,1:T(8,128)(2,1)S(1)}, u32[]{:S(2)}, u32[]{:S(2)}) async-start(bf16[2,12,96,8,64]{2,4,3,0,1:T(8,128)(2,1)} %bitcast.72), calls=%async_computation | async-start | bytes 6291456 | tf_op jit(solution)/shard_map/all_to_all | solution.py:29
  172.9 3.8 %copy-start.4 = (bf16[288,512]{0,1:T(8,128)(2,1)S(1)}, bf16[288,512]{0,1:T(8,128)(2,1)}, u32[]{:S(2)}) copy-start(bf16[288,512]{0,1:T(8,128)(2,1)} %copy-done.3) | copy-start | bytes 884740
  180.8 3.8 %copy-start.2 = (bf16[288,512]{0,1:T(8,128)(2,1)S(1)}, bf16[288,512]{0,1:T(8,128)(2,1)}, u32[]{:S(2)}) copy-start(bf16[288,512]{0,1:T(8,128)(2,1)} %copy-done.1) | copy-start | bytes 884740
  180.8 4.2 %copy-start.5 = (f32[8,256,64]{1,2,0:T(8,128)S(1)}, f32[8,256,64]{1,2,0:T(8,128)}, u32[]{:S(2)}) copy-start(f32[8,256,64]{1,2,0:T(8,128)} %fusion.34) | copy-start | bytes 1572868
  246.8 18.2 %all-to-all-start.5 = ((f32[8,64,256]{2,1,0:T(8,128)}), f32[8,64,256]{2,1,0:T(8,128)S(1)}, u32[]{:S(2)}, u32[]{:S(2)}) async-start(f32[8,64,256]{2,1,0:T(8,128)} %broadcast_in_dim.9), calls=%async_computation.5 | async-start | bytes 1048576 | tf_op jit(solution)/shard_map/all_to_all | solution.py:54

commit v9 on v5

--- a/solution.py
+++ b/solution.py
@@ -5,6 +5,7 @@
 DP = ("y", "zh", "core")
 BLK = ("zl", "x")
 DP_ORDER = ("core", "y", "zh")
+GROUPS, HALVES = 12, 2
 
 gelu_coef = 0.7978845608028654
 cubic_coef = 0.044715
@@ -21,11 +22,23 @@
 
 
 def to_tokens(panel):
-    return lax.all_to_all(panel, BLK, split_axis=1, concat_axis=2, tiled=True)
+    pair, rows, blocks, hidden = panel.shape
+    part = hidden // HALVES
+    groups = GROUPS // HALVES
+    panel = panel.reshape(pair, groups, rows // groups, blocks, HALVES, part).transpose(0, 1, 4, 2, 3, 5)
+    panel = panel.reshape(pair, GROUPS, rows // groups, blocks, part)
+    panel = lax.all_to_all(panel, BLK, split_axis=1, concat_axis=3, tiled=True)
+    return panel.reshape(pair, rows // groups, blocks * GROUPS, part)
 
 
 def to_blocks(panel):
-    return lax.all_to_all(panel, BLK, split_axis=2, concat_axis=1, tiled=True)
+    pair, rows, width, part = panel.shape
+    blocks = width // GROUPS
+    groups = GROUPS // HALVES
+    panel = panel.reshape(pair, rows, GROUPS, blocks, part).transpose(0, 2, 1, 3, 4)
+    panel = lax.all_to_all(panel, BLK, split_axis=1, concat_axis=1, tiled=True)
+    panel = panel.reshape(pair, groups, HALVES, rows, blocks, part).transpose(0, 1, 3, 4, 2, 5)
+    return panel.reshape(pair, groups * rows, blocks, HALVES * part)
 
 
 def dp_sum(total, sizes):
@@ -57,6 +70,10 @@
     grad_mixed = jnp.einsum("tqk,qkc->tqc", outgrads, down_last, preferred_element_type=flt).astype(
         half
     )
+    part = up_mix.shape[0] // HALVES
+    column = lax.rem(lax.axis_index("x"), HALVES) * part
+    up_mix = lax.dynamic_slice_in_dim(up_mix, column, part, axis=0)
+    down_mix = lax.dynamic_slice_in_dim(down_mix, column, part, axis=0)
     first_tok, grad_mixed_tok = to_tokens(jnp.stack([first, grad_mixed]))
     pre_tok = jnp.einsum("trc,csr->tsc", first_tok, up_mix, preferred_element_type=flt).astype(half)
     hidden_f, slope = gelu_pair(pre_tok.astype(flt))

time: 222 us -> 228 us (1.027)
  local copies, waits for them, and re-layouts: 35.9 us -> 50.7 us
  matrix products: 28.6 us -> 19 us
  waiting for transfers between devices: 26.4 us -> 29 us
  other arithmetic: 5.32 us -> 2.95 us
    unnamed x18 -> x24, local copies, waits for them, and re-layouts: 21.5 us -> 15.9 us
    dynamic_slice x0 -> x1, local copies, waits for them, and re-layouts: none -> 5.36 us  [shards(): up_mix = lax.dynamic_slice_in_dim(up_mix, column, part, axis=0)]
    convert_element_type x0 -> x2, local copies, waits for them, and re-layouts: none -> 4.09 us  [the longest x1 2.05 us: shards(): grad_first_tok = jnp.einsum('tsc,csr->trc', grad_pre_tok, up_mix, preferr...]
    dot_general x1, matrix products: 7.47 us -> 3.49 us  [shards(): jnp.einsum('tsc,cqs->tqc', hidden_tok, down_mix, preferred_element_type=flt)]
    another operation x5 -> x7, local copies, waits for them, and re-layouts: 6.4 us -> 10.3 us  [shards(): first_tok, grad_mixed_tok = to_tokens(jnp.stack([first, grad_mixed]))]
    another operation x4 -> x5, local copies, waits for them, and re-layouts: 5.03 us -> 8.62 us  [shards(): mixed, grad_first = to_blocks(jnp.stack([mixed_tok, grad_first_tok]))]
    dot_general x1, matrix products: 10.1 us -> 7.05 us  [shards(): jnp.einsum('tsc,csr->trc', grad_pre_tok, up_mix, preferred_element_type=flt)]
    all_to_all x1, waiting for transfers between devices: 15 us -> 17.6 us  [to_tokens(): panel = lax.all_to_all(panel, BLK, split_axis=1, concat_axis=3, tiled=True)]
  transfers between devices with their start and end apart: 2 -> 2, of which waited for: 2 -> 2; matrix products, arithmetic and copies ran while one was open for 9% -> 8% of each run, Pallas kernels for 0% -> 0%
where the time goes in v9:
time: 228 us; the launch traced here: 227 us
  blocking collectives  113 us (50%)
  local copies, waits for them, and re-layouts  50.7 us (22%)
  waiting for transfers between devices  29 us (13%)
  matrix products  19 us (8%)
  starting transfers between devices  11.3 us (5%)
  other arithmetic  2.95 us (1%)
    all_to_all x1, blocking collectives, to_blocks(): panel = lax.all_to_all(panel, BLK, split_axis=1, concat_axis=1, tiled=True)  47.8 us
    all_to_all x2, blocking collectives, dp_sum(): lax.all_to_all(total.reshape(count, -1, lanes), axis, 0, 0, tiled=True)  29.8 us
    all_to_all x1, blocking collectives, dp_sum(): total = lax.all_to_all(spread, DP_ORDER[-1], 0, 0, tiled=True).sum(axis=0)  28.1 us
    all_to_all x1, waiting for transfers between devices, to_tokens(): panel = lax.all_to_all(panel, BLK, split_axis=1, concat_axis=3, tiled=True)  17.6 us
    unnamed x24, local copies, waits for them, and re-layouts  15.9 us
    all_to_all x1, waiting for transfers between devices, dp_sum(): total = lax.all_to_all(spread, axis, 0, 0, tiled=True).reshape(-1, lanes)  11.4 us
    another operation x7, local copies, waits for them, and re-layouts, shards(): first_tok, grad_mixed_tok = to_tokens(jnp.stack([first, grad_mixed]))  10.3 us
    another operation x5, local copies, waits for them, and re-layouts, shards(): mixed, grad_first = to_blocks(jnp.stack([mixed_tok, grad_first_tok]))  8.62 us
  transfers between devices with their start and end apart: 2, of which 2 were waited for; matrix products, arithmetic and copies ran while one was open for 8% of the time, Pallas kernels for 0%

profile of v9, /device:TPU:7, one launch (start us, length us, event | category | flops | bytes accessed | tf_op | source)
XLA Modules:
  0.0 227.0 jit_solution(8857564223431193581)
XLA Ops:
  0.6 1.2 copy.55
  1.9 1.3 copy.56
  3.2 0.7 copy-done.3
  3.9 1.5 fusion.29
  5.7 1.8 copy.58
  7.5 0.5 fusion.28
  8.4 0.8 copy.57
  9.2 0.5 copy-done.2
  9.9 1.5 copy.59
  11.4 7.8 %all-to-all-start = ((bf16[2,12,48,8,128]{4,3,2,0,1:T(8,128)(2,1)}), bf16[2,12,48,8,128]{4,3,2,0,1:T(8,128)(2,1)}, u32[]{:S(2)}, u32[]{:S(2)}) async-start(bf16[2,12,48,8,128]{4,3,2,0,1:T(8,128)(2,1)} %copy.59), calls=%async_computation | async-start | bytes 4718592 | tf_op jit(solution)/shard_map/all_to_all | solution.py:30
  19.3 5.4 %constant_dynamic-slice_fusion = (bf16[128,96,96]{0,2,1:T(8,128)(2,1)}, bf16[128,96,96]{0,2,1:T(8,128)(2,1)}) fusion(bf16[256,96,96]{0,2,1:T(8,128)(2,1)} %param.8, s32[]{:T(128)S(6)} %select_n.4, bf16[256,96,96]{0,2,1:T(8,128)(2,1)} %param.9), kind=kLoop, calls=%fused_computation.41 | loop fusion | bytes 9437188 | tf_op jit(solution)/shard_map/dynamic_slice | solution.py:75
  24.6 3.5 %copy.72 = bf16[128,96,96]{2,1,0:T(8,128)(2,1)S(1)} copy(bf16[128,96,96]{0,2,1:T(8,128)(2,1)} %get-tuple-element.26) | data formatting | bytes 4718592
  28.2 4.8 %copy.71 = bf16[128,96,96]{2,1,0:T(8,128)(2,1)} copy(bf16[128,96,96]{0,2,1:T(8,128)(2,1)} %get-tuple-element.27) | data formatting | bytes 4718592
  32.9 17.6 %all-to-all-done = bf16[2,12,48,8,128]{4,3,2,0,1:T(8,128)(2,1)} async-done(((bf16[2,12,48,8,128]{4,3,2,0,1:T(8,128)(2,1)}), bf16[2,12,48,8,128]{4,3,2,0,1:T(8,128)(2,1)}, u32[]{:S(2)}, u32[]{:S(2)}) %all-to-all-start) | async-done | bytes 2359328 | tf_op jit(solution)/shard_map/all_to_all | solution.py:30
  50.6 2.1 copy.74
  52.6 1.6 slice_bitcast_fusion
  54.2 2.7 %copy.63 = bf16[48,96,128]{1,0,2:T(8,128)(2,1)} copy(bf16[48,96,128]{2,1,0:T(8,128)(2,1)} %get-tuple-element.22) | data formatting | bytes 2359296 | tf_op jit(solution)/shard_map/unstack | solution.py:77
  56.9 2.8 %copy.61 = bf16[48,96,128]{1,0,2:T(8,128)(2,1)} copy(bf16[48,96,128]{2,1,0:T(8,128)(2,1)} %get-tuple-element.23) | data formatting | bytes 2359296 | tf_op jit(solution)/shard_map/unstack | solution.py:77
  59.7 3.8 %convolution_convert_fusion.3 = bf16[128,96,48]{1,2,0:T(8,128)(2,1)S(1)} fusion(bf16[128,96,96]{2,1,0:T(8,128)(2,1)S(1)} %copy.72, bf16[48,96,128]{1,0,2:T(8,128)(2,1)} %copy.61), kind=kOutput, calls=%fused_computation.20 | convolution fusion | flops 113836032 | bytes 4718592 | tf_op jit(solution)/shard_map/trc,csr->tsc/dot_general | solution.py:78
  63.5 1.2 copy-done.8
  64.7 3.5 %fusion.22 = bf16[48,96,128]{1,0,2:T(8,128)(2,1)} fusion(bf16[128,96,96]{2,1,0:T(8,128)(2,1)S(1)} %copy-done.7, bf16[128,96,48]{1,2,0:T(8,128)(2,1)S(1)} %convolution_convert_fusion.3), kind=kOutput, calls=%fused_computation.32 | convolution fusion | flops 119734272 | bytes 4718592 | tf_op jit(solution)/shard_map/tsc,cqs->tqc/dot_general | solution.py:81
  68.2 7.1 %fusion.25 = bf16[48,96,128]{1,0,2:T(8,128)(2,1)} fusion(bf16[128,96,96]{2,1,0:T(8,128)(2,1)S(1)} %copy.72, bf16[128,96,48]{1,2,0:T(8,128)(2,1)} %copy-done.8, bf16[48,96,128]{1,0,2:T(8,128)(2,1)} %copy.63, bf16[128,96,96]{2,1,0:T(8,128)(2,1)} %copy.71), kind=kOutput, calls=%fused_computation.33 | convolution fusion | flops 240058368 | bytes 8257536 | tf_op jit(solution)/shard_map/tsc,csr->trc/dot_general | solution.py:88
  75.2 2.0 copy.62
  77.3 2.1 copy.64
  79.6 0.6 copy.65
  80.2 47.8 %all_to_all.45 = bf16[2,12,48,8,128]{4,3,2,0,1:T(8,128)(2,1)S(1)} all-to-all(bf16[2,12,48,8,128]{4,3,2,0,1:T(8,128)(2,1)S(1)} %copy.65), channel_id=1, replica_groups=mesh['y'=8,'zh'=4,'core'=2,'zl'=3,'x'=4] {'zl','x'}, dimensions={1} | all-to-all | bytes 4718592 | tf_op jit(solution)/shard_map/all_to_all | solution.py:39
  128.2 1.2 fusion.39
  129.5 1.2 copy.68
  130.7 0.8 unstack.31
  131.5 0.4 fusion.41
  131.9 0.9 copy-done.1
  132.8 2.2 copy.67
  135.0 3.1 %unstack.29 = bf16[288,8,256]{2,0,1:T(8,128)(2,1)S(1)} reshape(bf16[1,6,48,8,2,128]{5,4,2,1,3,0:T(2,128)(2,1)} %copy.67) | data formatting | bytes 2359296 | tf_op jit(solution)/shard_map/unstack | solution.py:91
  138.2 0.4 fusion.42
  138.6 6.9 %all_to_all.46 = f32[2,512,256]{2,1,0:T(8,128)} all-to-all(f32[2,512,256]{2,1,0:T(8,128)S(1)} %bitcast.106), channel_id=1, replica_groups=mesh['y'=8,'zh'=4,'core'=2,'zl'=3,'x'=4] {'core'}, dimensions={0} | all-to-all | bytes 2097152 | tf_op jit(solution)/shard_map/all_to_all | solution.py:48
  145.6 1.4 reduce_sum.27
  146.9 22.9 %all_to_all.47 = f32[8,64,256]{2,1,0:T(8,128)} all-to-all(f32[8,64,256]{2,1,0:T(8,128)S(1)} %bitcast.112), channel_id=1, replica_groups=mesh['y'=8,'zh'=4,'core'=2,'zl'=3,'x'=4] {'y'}, dimensions={0} | all-to-all | bytes 1048576 | tf_op jit(solution)/shard_map/all_to_all | solution.py:48
  169.8 1.1 reduce_sum.28
  170.9 28.1 %all_to_all.48 = f32[4,64,256]{2,1,0:T(8,128)S(1)} all-to-all(f32[4,64,256]{2,1,0:T(8,128)S(1)} %broadcast_in_dim.8), channel_id=1, replica_groups=mesh['y'=8,'zh'=4,'core'=2,'zl'=3,'x'=4] {'zh'}, dimensions={0} | all-to-all | bytes 524288 | tf_op jit(solution)/shard_map/all_to_all | solution.py:52
  199.0 0.8 broadcast_in_dim.9
  199.9 3.5 %all-to-all-start.5 = ((f32[8,64,256]{2,1,0:T(8,128)}), f32[8,64,256]{2,1,0:T(8,128)S(1)}, u32[]{:S(2)}, u32[]{:S(2)}) async-start(f32[8,64,256]{2,1,0:T(8,128)} %broadcast_in_dim.9), calls=%async_computation.5 | async-start | bytes 1048576 | tf_op jit(solution)/shard_map/all_to_all | solution.py:56
  203.4 0.5 convolution_convert_fusion.6
  203.9 0.9 copy.70
  204.7 1.4 convolution_convert_fusion.7
  206.2 0.9 copy.69
  207.1 11.4 %all-to-all-done.5 = f32[8,64,256]{2,1,0:T(8,128)S(1)} async-done(((f32[8,64,256]{2,1,0:T(8,128)}), f32[8,64,256]{2,1,0:T(8,128)S(1)}, u32[]{:S(2)}, u32[]{:S(2)}) %all-to-all-start.5) | async-done | bytes 524320 | tf_op jit(solution)/shard_map/all_to_all | solution.py:56
  218.5 7.5 %all_to_all.49 = f32[2,512,256]{2,1,0:T(8,128)S(1)} all-to-all(f32[2,512,256]{2,1,0:T(8,128)S(1)} %broadcast_in_dim.22), channel_id=1, replica_groups=mesh['y'=8,'zh'=4,'core'=2,'zl'=3,'x'=4] {'core'}, dimensions={0} | all-to-all | bytes 2097152 | tf_op jit(solution)/shard_map/all_to_all | solution.py:56
  226.0 1.0 fusion.40
  (23 shorter events, 1.5 us)
Async XLA Ops:
  0.6 6.9 %copy-start = (bf16[8,64,256]{2,1,0:T(8,128)(2,1)S(1)}, bf16[8,64,256]{2,1,0:T(8,128)(2,1)}, u32[]{:S(2)}) copy-start(bf16[8,64,256]{2,1,0:T(8,128)(2,1)} %param.7) | copy-start | bytes 786436
  1.9 5.7 %copy-start.5 = (bf16[288,512]{0,1:T(8,128)(2,1)}, bf16[288,512]{0,1:T(8,128)(2,1)S(1)}, u32[]{:S(2)}) copy-start(bf16[288,512]{0,1:T(8,128)(2,1)S(1)} %copy.55) | copy-start | bytes 884740
  3.2 0.7 copy-start.3
  8.4 1.3 copy-start.2
  11.4 39.1 %all-to-all-start = ((bf16[2,12,48,8,128]{4,3,2,0,1:T(8,128)(2,1)}), bf16[2,12,48,8,128]{4,3,2,0,1:T(8,128)(2,1)}, u32[]{:S(2)}, u32[]{:S(2)}) async-start(bf16[2,12,48,8,128]{4,3,2,0,1:T(8,128)(2,1)} %copy.59), calls=%async_computation | async-start | bytes 4718592 | tf_op jit(solution)/shard_map/all_to_all | solution.py:30
  59.7 5.0 %copy-start.7 = (bf16[128,96,96]{2,1,0:T(8,128)(2,1)S(1)}, bf16[128,96,96]{2,1,0:T(8,128)(2,1)}, u32[]{:S(2)}) copy-start(bf16[128,96,96]{2,1,0:T(8,128)(2,1)} %copy.71) | copy-start | bytes 7077892
  63.5 1.2 copy-start.8
  129.5 2.0 copy-start.6
  131.5 1.3 copy-start.1
  132.8 5.4 %copy-start.4 = (bf16[288,512]{0,1:T(8,128)(2,1)S(1)}, bf16[288,512]{0,1:T(8,128)(2,1)}, u32[]{:S(2)}) copy-start(bf16[288,512]{0,1:T(8,128)(2,1)} %copy-done.3) | copy-start | bytes 884740
  199.9 18.6 %all-to-all-start.5 = ((f32[8,64,256]{2,1,0:T(8,128)}), f32[8,64,256]{2,1,0:T(8,128)S(1)}, u32[]{:S(2)}, u32[]{:S(2)}) async-start(f32[8,64,256]{2,1,0:T(8,128)} %broadcast_in_dim.9), calls=%async_computation.5 | async-start | bytes 1048576 | tf_op jit(solution)/shard_map/all_to_all | solution.py:56
